TPU v7x, 256 devices: a whole 4x4x8 slice. The times are simulated.
256 devices in a mesh: row: 8 (over x_lo, y), col: 32 (over z, x_hi, core).
Axes of the slice: x: 4 (x_hi: 2, x_lo: 2; x = x_hi * 2 + x_lo), y: 4, z: 8, core: 2. Of those that a mesh axis runs over, the one named last changes fastest.
Arguments:
- a_blocks: float32 [32, 8, 32, 4096], P('col', 'row'), may hold values from -0.25 to 0.25
- a_rows: int32 [32, 8, 32], P('col', 'row'), may hold values from 0 to 32, as said below
- a_slots: int32 [32, 8, 32], P('col', 'row'), may hold values from 0 to 23, as said below
- b_stripes: float32 [192, 64, 1024], P('col', None, 'row'), may hold values from -6 to 6
Outputs:
- product: float32 [65536, 1024], P('col', 'row')
Inputs may be any that keep to these rules, and one draw needn't show every extreme that they name: `a_rows`: in each group and panel the used slots (row below 32) come first, in rising order of the pair (row, stripe), no pair twice; the remaining slots hold 32. In every draw one group has all 32 slots of all its panels used; in the others each panel uses between a quarter and five eighths of them. `a_slots`: stripe of each slot within its panel; empty slots hold 0.
All inputs are finite; a program needn't handle non-finite values.
Results may differ from a plain program's by a relative error of at most 0.0003.
Values sent between devices are 32-bit elements; how exact they have to be, the bound alone decides.
No kernel may reach another device: no remote copies, remote signals or barrier semaphores. Data moves between devices by JAX's collectives and lax.ppermute only.
A program may use at most 64 MiB of HBM per device.

v0:
```python
import functools

import jax
import jax.numpy as jnp
from jax import lax
from jax.experimental import pallas as pl
from jax.experimental.pallas import tpu as pltpu
from jax.sharding import Mesh

from jax.sharding import PartitionSpec as P

BLK = 64
MB = 32

AXES = ("xl", "y", "z", "xh", "core")
ROW = ("xl", "y")
COL = ("z", "xh", "core")


def swap(block, axis):
    return lax.ppermute(block, axis, [(0, 1), (1, 0)])


def shift(block, axis, distance):
    n = lax.axis_size(axis)
    return lax.ppermute(block, axis, [(i, (i + distance) % n) for i in range(n)])


def gather_a(a_own):
    n_y = lax.axis_size("y")
    xl = lax.axis_index("xl")
    y = lax.axis_index("y")
    a_x = swap(a_own, "xl")
    bundle = jnp.stack([a_own, a_x])
    from_minus = shift(bundle, "y", 1)
    from_plus = shift(bundle, "y", -1)
    far_a = shift(from_plus[0], "y", -1)
    far_b = shift(from_minus[1], "y", 1)
    pieces = [a_own[None], a_x[None], from_minus, from_plus, far_a[None], far_b[None]]
    ys = [y, y, y - 1, y - 1, y + 1, y + 1, y + 2, y + 2]
    xls = [xl, 1 - xl] * 4
    pid = jnp.stack([xls[k] * n_y + (ys[k] % n_y) for k in range(8)]).astype(jnp.int32)
    return pieces, pid


def gather_b(b_own):
    n_z = lax.axis_size("z")
    pair = jnp.stack([b_own, swap(b_own, "xh")])
    by_offset = [None] * n_z
    by_offset[0] = pair
    up = pair
    down = pair
    half = n_z // 2
    for d in range(1, half):
        up = shift(up, "z", -1)
        down = shift(down, "z", 1)
        by_offset[d] = up
        by_offset[n_z - d] = down
    far_up = shift(up[0], "z", -1)
    far_down = shift(down[1], "z", 1)
    by_offset[half] = jnp.stack([far_up, far_down])
    mine = jnp.stack(by_offset)
    other = jnp.stack([swap(piece, "core") for piece in by_offset])
    return mine, other


def product_kernel(n_pieces, index_ref, rows_ref, *refs):
    a_refs = refs[:n_pieces]
    mine_ref, other_ref, out_ref, acc_ref = refs[n_pieces:]
    acc_ref[...] = jnp.zeros_like(acc_ref)
    blocks = out_ref.shape[0]
    stripes = mine_ref.shape[0]

    panel = 0
    for a_ref in a_refs:
        for j in range(a_ref.shape[0]):
            n_pairs = a_ref.shape[1]
            base = panel * 2 * n_pairs

            def one_pair(t, carry, a_ref=a_ref, j=j, base=base):
                pair = a_ref[j, t]
                pair_hi = pair.astype(jnp.bfloat16)
                pair_lo = (pair - pair_hi.astype(jnp.float32)).astype(jnp.bfloat16)
                for u in range(2):
                    g = base + 2 * t + u
                    row = jnp.minimum(rows_ref[g], blocks)
                    index = index_ref[g]
                    local = index % stripes
                    right = jnp.where(index < stripes, mine_ref[local], other_ref[local])
                    right_hi = right.astype(jnp.bfloat16)
                    right_lo = (right - right_hi.astype(jnp.float32)).astype(jnp.bfloat16)
                    zeros = jnp.zeros_like(right_hi)
                    pieces_hi = [right_hi, zeros] if u == 0 else [zeros, right_hi]
                    pieces_lo = [right_lo, zeros] if u == 0 else [zeros, right_lo]
                    right_hi = jnp.concatenate(pieces_hi, axis=0)
                    right_lo = jnp.concatenate(pieces_lo, axis=0)
                    term = jnp.dot(pair_hi, right_hi, preferred_element_type=jnp.float32)
                    term += jnp.dot(pair_hi, right_lo, preferred_element_type=jnp.float32)
                    term += jnp.dot(pair_lo, right_hi, preferred_element_type=jnp.float32)
                    acc_ref[row] += term
                return carry

            lax.fori_loop(0, n_pairs, one_pair, 0, unroll=4)
            panel += 1
    out_ref[...] = acc_ref[:blocks]


def product(index, rows, pieces, mine, other):
    _, n_pairs, blk, _ = pieces[0].shape
    n_panels = sum(piece.shape[0] for piece in pieces)
    columns = mine.shape[2]
    vmem = pl.BlockSpec(memory_space=pltpu.VMEM)
    smem = pl.BlockSpec(memory_space=pltpu.SMEM)
    return pl.pallas_call(
        functools.partial(product_kernel, len(pieces)),
        out_shape=jax.ShapeDtypeStruct((MB, blk, columns), jnp.float32),
        in_specs=[smem, smem] + [vmem] * (len(pieces) + 2),
        out_specs=vmem,
        scratch_shapes=[pltpu.VMEM((MB + 1, blk, columns), jnp.float32)],
        compiler_params=pltpu.CompilerParams(vmem_limit_bytes=48 * 1024 * 1024),
        cost_estimate=pl.CostEstimate(
            flops=2 * 2 * n_panels * n_pairs * blk * blk * columns,
            bytes_accessed=4 * (sum(piece.size for piece in pieces) + 2 * mine.size + MB * blk * columns),
            transcendentals=0,
        ),
    )(index, rows, *pieces, mine, other)


def as_pairs(panel):
    slots = panel.shape[0]
    blocks = panel.reshape(slots // 2, 2, BLK, BLK)
    return jnp.swapaxes(blocks, 1, 2).reshape(slots // 2, BLK, 2 * BLK)


def shards_body(a_blocks, a_rows, a_slots, b_stripes):
    n_z = lax.axis_size("z")
    z = lax.axis_index("z")
    columns = b_stripes.shape[2]

    ints = jnp.stack([a_rows[0, 0], a_slots[0, 0]])
    ints_k, _ = gather_a(ints)
    ints_k = jnp.concatenate(ints_k)
    a_pieces, pid = gather_a(as_pairs(a_blocks[0, 0]))
    mine, other = gather_b(b_stripes)
    mine = mine.reshape(-1, BLK, columns)
    other = other.reshape(-1, BLK, columns)

    rows = ints_k[:, 0]
    slots = ints_k[:, 1]
    d = (pid[:, None] - z) % n_z
    core_rel = (slots // 6) % 2 ^ lax.axis_index("core")
    xh_rel = (slots // 12) ^ lax.axis_index("xh")
    index = ((core_rel * n_z + d) * 2 + xh_rel) * 6 + slots % 6
    out = product(index.reshape(-1), rows.reshape(-1), a_pieces, mine, other)
    return out.reshape(MB * BLK, columns)


def solution(mesh):
    fine = Mesh(mesh.devices.reshape(2, 4, 8, 2, 2), AXES)
    return jax.shard_map(
        shards_body,
        mesh=fine,
        in_specs=(
            P(COL, ROW, None, None),
            P(COL, ROW, None),
            P(COL, ROW, None),
            P(COL, None, ROW),
        ),
        out_specs=P(COL, ROW),
        check_vma=False,
    )
```

profile of v0, /device:TPU:2, one launch (start us, length us, event | category | flops | bytes accessed | tf_op | source)
XLA Modules:
  0.0 104.8 jit_solution(89408675397637009)
XLA Ops:
  0.7 2.2 %collective-permute-start = (s32[2,32]{1,0:T(2,128)S(1)}, s32[2,32]{1,0:T(2,128)S(1)}, u32[]{:S(2)}, u32[]{:S(2)}) collective-permute-start(s32[2,32]{1,0:T(2,128)S(1)} %get-tuple-element.12), channel_id=1, source_target_pairs={{0,128},{128,0},{1,129},{129,1},{2,130},{130,2},{3,131},{131,3},{4... | collective-permute-start | bytes 776 | tf_op jit(solution)/shard_map/ppermute | solution.py:21
  3.7 1.5 %reshape_squeeze.7 = f32[16,2,64,64]{3,2,1,0:T(8,128)S(1)} reshape(f32[1,1,32,4096]{3,2,1,0:T(8,128)} %param.4) | data formatting | bytes 1048576 | tf_op jit(solution)/shard_map/reshape;squeeze | solution.py:131
  6.6 1.9 %collective-permute-start.5 = (f32[16,64,128]{2,1,0:T(8,128)S(1)}, f32[16,64,128]{2,1,0:T(8,128)S(1)}, u32[]{:S(2)}, u32[]{:S(2)}) collective-permute-start(f32[16,64,128]{2,1,0:T(8,128)S(1)} %reshape.111), channel_id=1, source_target_pairs={{0,128},{128,0},{1,129},{129,1},{2,130},{130,2},{3,131},{131,3},{4... | collective-permute-start | bytes 1572872 | tf_op jit(solution)/shard_map/ppermute | solution.py:21
  9.3 1.7 %collective-permute-start.1 = (s32[2,2,32]{2,1,0:T(2,128)S(1)}, s32[2,2,32]{2,1,0:T(2,128)S(1)}, u32[]{:S(2)}, u32[]{:S(2)}) collective-permute-start(s32[2,2,32]{2,1,0:T(2,128)S(1)} %pad_add_fusion), channel_id=1, source_target_pairs={{0,32},{32,64},{64,96},{96,0},{1,33},{33,65},{65,97},{97,1},{2,34}... | collective-permute-start | bytes 1544 | tf_op jit(solution)/shard_map/ppermute | solution.py:26
  11.0 1.7 %collective-permute-start.2 = (s32[2,2,32]{2,1,0:T(2,128)S(1)}, s32[2,2,32]{2,1,0:T(2,128)S(1)}, u32[]{:S(2)}, u32[]{:S(2)}) collective-permute-start(s32[2,2,32]{2,1,0:T(2,128)S(1)} %pad_add_fusion), channel_id=1, source_target_pairs={{0,96},{32,0},{64,32},{96,64},{1,97},{33,1},{65,33},{97,65},{2,98}... | collective-permute-start | bytes 1544 | tf_op jit(solution)/shard_map/ppermute | solution.py:26
  12.7 1.9 %collective-permute-done.2 = s32[2,2,32]{2,1,0:T(2,128)S(1)} collective-permute-done((s32[2,2,32]{2,1,0:T(2,128)S(1)}, s32[2,2,32]{2,1,0:T(2,128)S(1)}, u32[]{:S(2)}, u32[]{:S(2)}) %collective-permute-start.2) | collective-permute-done | bytes 544 | tf_op jit(solution)/shard_map/ppermute | solution.py:26
  14.6 2.9 %collective-permute-start.3 = (s32[2,32]{1,0:T(2,128)S(1)}, s32[2,32]{1,0:T(2,128)S(1)}, u32[]{:S(2)}, u32[]{:S(2)}) collective-permute-start(s32[2,32]{1,0:T(2,128)S(1)} %slice_bitcast_fusion.5), channel_id=1, source_target_pairs={{0,96},{32,0},{64,32},{96,64},{1,97},{33,1},{65,33},{97,65},{2,98}... | collective-permute-start | bytes 776 | tf_op jit(solution)/shard_map/ppermute | solution.py:26
  18.8 3.5 %collective-permute-done.4 = s32[2,32]{1,0:T(2,128)S(1)} collective-permute-done((s32[2,32]{1,0:T(2,128)S(1)}, s32[2,32]{1,0:T(2,128)S(1)}, u32[]{:S(2)}, u32[]{:S(2)}) %collective-permute-start.4) | collective-permute-done | bytes 288 | tf_op jit(solution)/shard_map/ppermute | solution.py:26
  22.9 5.9 %collective-permute-start.11 = (f32[2,6,64,128]{3,2,1,0:T(8,128)S(1)}, f32[2,6,64,128]{3,2,1,0:T(8,128)S(1)}, u32[]{:S(2)}, u32[]{:S(2)}) collective-permute-start(f32[2,6,64,128]{3,2,1,0:T(8,128)S(1)} %pad_maximum_fusion.1), channel_id=1, source_target_pairs={{0,28},{4,0},{8,4},{12,8},{16,12},{20,16},{24,20},{28,24},{1,29},{... | collective-permute-start | bytes 1179656 | tf_op jit(solution)/shard_map/ppermute | solution.py:26
  29.1 2.0 %collective-permute-start.6 = (f32[2,16,64,128]{3,2,1,0:T(8,128)S(1)}, f32[2,16,64,128]{3,2,1,0:T(8,128)S(1)}, u32[]{:S(2)}, u32[]{:S(2)}) collective-permute-start(f32[2,16,64,128]{3,2,1,0:T(8,128)S(1)} %pad_maximum_fusion), channel_id=1, source_target_pairs={{0,32},{32,64},{64,96},{96,0},{1,33},{33,65},{65,97},{97,1},{2,34}... | collective-permute-start | bytes 3145736 | tf_op jit(solution)/shard_map/ppermute | solution.py:26
  31.1 3.0 %collective-permute-done.11 = f32[2,6,64,128]{3,2,1,0:T(8,128)S(1)} collective-permute-done((f32[2,6,64,128]{3,2,1,0:T(8,128)S(1)}, f32[2,6,64,128]{3,2,1,0:T(8,128)S(1)}, u32[]{:S(2)}, u32[]{:S(2)}) %collective-permute-start.11) | collective-permute-done | bytes 393248 | tf_op jit(solution)/shard_map/ppermute | solution.py:26
  34.1 3.7 %collective-permute-start.12 = (f32[2,6,64,128]{3,2,1,0:T(8,128)S(1)}, f32[2,6,64,128]{3,2,1,0:T(8,128)S(1)}, u32[]{:S(2)}, u32[]{:S(2)}) collective-permute-start(f32[2,6,64,128]{3,2,1,0:T(8,128)S(1)} %collective-permute-done.11), channel_id=1, source_target_pairs={{0,28},{4,0},{8,4},{12,8},{16,12},{20,16},{24,20},{28,24},{1,29},{... | collective-permute-start | bytes 1179656 | tf_op jit(solution)/shard_map/ppermute | solution.py:26
  37.8 3.7 %collective-permute-done.15 = f32[2,6,64,128]{3,2,1,0:T(8,128)S(1)} collective-permute-done((f32[2,6,64,128]{3,2,1,0:T(8,128)S(1)}, f32[2,6,64,128]{3,2,1,0:T(8,128)S(1)}, u32[]{:S(2)}, u32[]{:S(2)}) %collective-permute-start.15) | collective-permute-done | bytes 393248 | tf_op jit(solution)/shard_map/ppermute | solution.py:26
  41.6 5.2 %collective-permute-done.12 = f32[2,6,64,128]{3,2,1,0:T(8,128)S(1)} collective-permute-done((f32[2,6,64,128]{3,2,1,0:T(8,128)S(1)}, f32[2,6,64,128]{3,2,1,0:T(8,128)S(1)}, u32[]{:S(2)}, u32[]{:S(2)}) %collective-permute-start.12) | collective-permute-done | bytes 393248 | tf_op jit(solution)/shard_map/ppermute | solution.py:26
  46.9 3.7 %collective-permute-start.13 = (f32[2,6,64,128]{3,2,1,0:T(8,128)S(1)}, f32[2,6,64,128]{3,2,1,0:T(8,128)S(1)}, u32[]{:S(2)}, u32[]{:S(2)}) collective-permute-start(f32[2,6,64,128]{3,2,1,0:T(8,128)S(1)} %collective-permute-done.12), channel_id=1, source_target_pairs={{0,28},{4,0},{8,4},{12,8},{16,12},{20,16},{24,20},{28,24},{1,29},{... | collective-permute-start | bytes 1179656 | tf_op jit(solution)/shard_map/ppermute | solution.py:26
  50.7 2.7 %collective-permute-done.16 = f32[2,6,64,128]{3,2,1,0:T(8,128)S(1)} collective-permute-done((f32[2,6,64,128]{3,2,1,0:T(8,128)S(1)}, f32[2,6,64,128]{3,2,1,0:T(8,128)S(1)}, u32[]{:S(2)}, u32[]{:S(2)}) %collective-permute-start.16) | collective-permute-done | bytes 393248 | tf_op jit(solution)/shard_map/ppermute | solution.py:26
  53.5 5.3 %collective-permute-done.13 = f32[2,6,64,128]{3,2,1,0:T(8,128)S(1)} collective-permute-done((f32[2,6,64,128]{3,2,1,0:T(8,128)S(1)}, f32[2,6,64,128]{3,2,1,0:T(8,128)S(1)}, u32[]{:S(2)}, u32[]{:S(2)}) %collective-permute-start.13) | collective-permute-done | bytes 393248 | tf_op jit(solution)/shard_map/ppermute | solution.py:26
  58.8 5.7 %collective-permute-done.17 = f32[2,6,64,128]{3,2,1,0:T(8,128)S(1)} collective-permute-done((f32[2,6,64,128]{3,2,1,0:T(8,128)S(1)}, f32[2,6,64,128]{3,2,1,0:T(8,128)S(1)}, u32[]{:S(2)}, u32[]{:S(2)}) %collective-permute-start.17) | collective-permute-done | bytes 393248 | tf_op jit(solution)/shard_map/ppermute | solution.py:26
  64.7 2.1 %collective-permute-start.18 = (f32[6,64,128]{2,1,0:T(8,128)S(1)}, f32[6,64,128]{2,1,0:T(8,128)S(1)}, u32[]{:S(2)}, u32[]{:S(2)}) collective-permute-start(f32[6,64,128]{2,1,0:T(8,128)S(1)} %slice_bitcast_fusion.2), channel_id=1, source_target_pairs={{0,4},{4,8},{8,12},{12,16},{16,20},{20,24},{24,28},{28,0},{1,5},{5... | collective-permute-start | bytes 589832 | tf_op jit(solution)/shard_map/ppermute | solution.py:26
  67.0 5.0 %collective-permute-done.14 = f32[6,64,128]{2,1,0:T(8,128)S(1)} collective-permute-done((f32[6,64,128]{2,1,0:T(8,128)S(1)}, f32[6,64,128]{2,1,0:T(8,128)S(1)}, u32[]{:S(2)}, u32[]{:S(2)}) %collective-permute-start.14) | collective-permute-done | bytes 196640 | tf_op jit(solution)/shard_map/ppermute | solution.py:26
  73.7 1.4 %collective-permute-done.23 = f32[2,6,64,128]{3,2,1,0:T(8,128)S(1)} collective-permute-done((f32[2,6,64,128]{3,2,1,0:T(8,128)S(1)}, f32[2,6,64,128]{3,2,1,0:T(8,128)S(1)}, u32[]{:S(2)}, u32[]{:S(2)}) %collective-permute-start.23) | collective-permute-done | bytes 393248 | tf_op jit(solution)/shard_map/ppermute | solution.py:21
  76.0 12.0 %collective-permute-done.8 = f32[16,64,128]{2,1,0:T(8,128)S(1)} collective-permute-done((f32[16,64,128]{2,1,0:T(8,128)S(1)}, f32[16,64,128]{2,1,0:T(8,128)S(1)}, u32[]{:S(2)}, u32[]{:S(2)}) %collective-permute-start.8) | collective-permute-done | bytes 524320 | tf_op jit(solution)/shard_map/ppermute | solution.py:26
  88.0 2.3 %collective-permute-done.9 = f32[16,64,128]{2,1,0:T(8,128)S(1)} collective-permute-done((f32[16,64,128]{2,1,0:T(8,128)S(1)}, f32[16,64,128]{2,1,0:T(8,128)S(1)}, u32[]{:S(2)}, u32[]{:S(2)}) %collective-permute-start.9) | collective-permute-done | bytes 524320 | tf_op jit(solution)/shard_map/ppermute | solution.py:26
  90.3 14.5 %shard_map.46 = f32[32,64,128]{2,1,0:T(8,128)} custom-call(s32[256]{0:T(256)S(1)} %fusion.5.index_ref, s32[256]{0:T(256)S(1)} %reshape_squeeze.6.rows_ref, f32[1,16,64,128]{3,2,1,0:T(8,128)S(1)} %broadcast_in_dim_reshape.3.refs_0_, f32[1,16,64,128]{3,2,1,0:T(8,128)S(1)} %bitcast.79, f32[2,16,64,128]{3,2,1,0:T(8,128)S(1)} %collective-permute-done.6.refs_2_, ...), custom_call_target="tpu_custom_call" | custom-call | flops 268435456 | bytes 11534336 | tf_op jit(solution)/shard_map/pallas_call | solution.py:114
  (91 shorter events, 8.9 us)
Async XLA Ops:
  0.7 8.6 %collective-permute-start = (s32[2,32]{1,0:T(2,128)S(1)}, s32[2,32]{1,0:T(2,128)S(1)}, u32[]{:S(2)}, u32[]{:S(2)}) collective-permute-start(s32[2,32]{1,0:T(2,128)S(1)} %get-tuple-element.12), channel_id=1, source_target_pairs={{0,128},{128,0},{1,129},{129,1},{2,130},{130,2},{3,131},{131,3},{4... | collective-permute-start | bytes 776 | tf_op jit(solution)/shard_map/ppermute | solution.py:21
  3.0 19.9 %collective-permute-start.10 = (f32[6,64,128]{2,1,0:T(8,128)}, f32[6,64,128]{2,1,0:T(8,128)S(1)}, u32[]{:S(2)}, u32[]{:S(2)}) collective-permute-start(f32[6,64,128]{2,1,0:T(8,128)} %param.7), channel_id=1, source_target_pairs={{0,2},{2,0},{1,3},{3,1},{4,6},{6,4},{5,7},{7,5},{8,10},{10,8},{9,1... | collective-permute-start | bytes 589832 | tf_op jit(solution)/shard_map/ppermute | solution.py:21
  6.6 22.3 %collective-permute-start.5 = (f32[16,64,128]{2,1,0:T(8,128)S(1)}, f32[16,64,128]{2,1,0:T(8,128)S(1)}, u32[]{:S(2)}, u32[]{:S(2)}) collective-permute-start(f32[16,64,128]{2,1,0:T(8,128)S(1)} %reshape.111), channel_id=1, source_target_pairs={{0,128},{128,0},{1,129},{129,1},{2,130},{130,2},{3,131},{131,3},{4... | collective-permute-start | bytes 1572872 | tf_op jit(solution)/shard_map/ppermute | solution.py:21
  9.3 8.1 %collective-permute-start.1 = (s32[2,2,32]{2,1,0:T(2,128)S(1)}, s32[2,2,32]{2,1,0:T(2,128)S(1)}, u32[]{:S(2)}, u32[]{:S(2)}) collective-permute-start(s32[2,2,32]{2,1,0:T(2,128)S(1)} %pad_add_fusion), channel_id=1, source_target_pairs={{0,32},{32,64},{64,96},{96,0},{1,33},{33,65},{65,97},{97,1},{2,34}... | collective-permute-start | bytes 1544 | tf_op jit(solution)/shard_map/ppermute | solution.py:26
  14.6 4.2 %collective-permute-start.3 = (s32[2,32]{1,0:T(2,128)S(1)}, s32[2,32]{1,0:T(2,128)S(1)}, u32[]{:S(2)}, u32[]{:S(2)}) collective-permute-start(s32[2,32]{1,0:T(2,128)S(1)} %slice_bitcast_fusion.5), channel_id=1, source_target_pairs={{0,96},{32,0},{64,32},{96,64},{1,97},{33,1},{65,33},{97,65},{2,98}... | collective-permute-start | bytes 776 | tf_op jit(solution)/shard_map/ppermute | solution.py:26
  17.5 4.8 %collective-permute-start.4 = (s32[2,32]{1,0:T(2,128)S(1)}, s32[2,32]{1,0:T(2,128)S(1)}, u32[]{:S(2)}, u32[]{:S(2)}) collective-permute-start(s32[2,32]{1,0:T(2,128)S(1)} %slice_bitcast_fusion.4), channel_id=1, source_target_pairs={{0,32},{32,64},{64,96},{96,0},{1,33},{33,65},{65,97},{97,1},{2,34}... | collective-permute-start | bytes 776 | tf_op jit(solution)/shard_map/ppermute | solution.py:26
  22.9 11.2 %collective-permute-start.11 = (f32[2,6,64,128]{3,2,1,0:T(8,128)S(1)}, f32[2,6,64,128]{3,2,1,0:T(8,128)S(1)}, u32[]{:S(2)}, u32[]{:S(2)}) collective-permute-start(f32[2,6,64,128]{3,2,1,0:T(8,128)S(1)} %pad_maximum_fusion.1), channel_id=1, source_target_pairs={{0,28},{4,0},{8,4},{12,8},{16,12},{20,16},{24,20},{28,24},{1,29},{... | collective-permute-start | bytes 1179656 | tf_op jit(solution)/shard_map/ppermute | solution.py:26
  28.8 5.3 %collective-permute-start.19 = (f32[2,6,64,128]{3,2,1,0:T(8,128)S(1)}, f32[2,6,64,128]{3,2,1,0:T(8,128)S(1)}, u32[]{:S(2)}, u32[]{:S(2)}) collective-permute-start(f32[2,6,64,128]{3,2,1,0:T(8,128)S(1)} %pad_maximum_fusion.1), channel_id=1, source_target_pairs={{0,1},{1,0},{2,3},{3,2},{4,5},{5,4},{6,7},{7,6},{8,9},{9,8},{10,11... | collective-permute-start | bytes 1179656 | tf_op jit(solution)/shard_map/ppermute | solution.py:21
  28.8 12.7 %collective-permute-start.15 = (f32[2,6,64,128]{3,2,1,0:T(8,128)S(1)}, f32[2,6,64,128]{3,2,1,0:T(8,128)S(1)}, u32[]{:S(2)}, u32[]{:S(2)}) collective-permute-start(f32[2,6,64,128]{3,2,1,0:T(8,128)S(1)} %pad_maximum_fusion.1), channel_id=1, source_target_pairs={{0,4},{4,8},{8,12},{12,16},{16,20},{20,24},{24,28},{28,0},{1,5},{5... | collective-permute-start | bytes 1179656 | tf_op jit(solution)/shard_map/ppermute | solution.py:26
  29.0 35.7 %collective-permute-start.7 = (f32[2,16,64,128]{3,2,1,0:T(8,128)S(1)}, f32[2,16,64,128]{3,2,1,0:T(8,128)S(1)}, u32[]{:S(2)}, u32[]{:S(2)}) collective-permute-start(f32[2,16,64,128]{3,2,1,0:T(8,128)S(1)} %pad_maximum_fusion), channel_id=1, source_target_pairs={{0,96},{32,0},{64,32},{96,64},{1,97},{33,1},{65,33},{97,65},{2,98}... | collective-permute-start | bytes 3145736 | tf_op jit(solution)/shard_map/ppermute | solution.py:26
  29.1 37.7 %collective-permute-start.6 = (f32[2,16,64,128]{3,2,1,0:T(8,128)S(1)}, f32[2,16,64,128]{3,2,1,0:T(8,128)S(1)}, u32[]{:S(2)}, u32[]{:S(2)}) collective-permute-start(f32[2,16,64,128]{3,2,1,0:T(8,128)S(1)} %pad_maximum_fusion), channel_id=1, source_target_pairs={{0,32},{32,64},{64,96},{96,0},{1,33},{33,65},{65,97},{97,1},{2,34}... | collective-permute-start | bytes 3145736 | tf_op jit(solution)/shard_map/ppermute | solution.py:26
  34.1 16.5 %collective-permute-start.20 = (f32[2,6,64,128]{3,2,1,0:T(8,128)S(1)}, f32[2,6,64,128]{3,2,1,0:T(8,128)S(1)}, u32[]{:S(2)}, u32[]{:S(2)}) collective-permute-start(f32[2,6,64,128]{3,2,1,0:T(8,128)S(1)} %collective-permute-done.11), channel_id=1, source_target_pairs={{0,1},{1,0},{2,3},{3,2},{4,5},{5,4},{6,7},{7,6},{8,9},{9,8},{10,11... | collective-permute-start | bytes 1179656 | tf_op jit(solution)/shard_map/ppermute | solution.py:21
  34.1 12.7 %collective-permute-start.12 = (f32[2,6,64,128]{3,2,1,0:T(8,128)S(1)}, f32[2,6,64,128]{3,2,1,0:T(8,128)S(1)}, u32[]{:S(2)}, u32[]{:S(2)}) collective-permute-start(f32[2,6,64,128]{3,2,1,0:T(8,128)S(1)} %collective-permute-done.11), channel_id=1, source_target_pairs={{0,28},{4,0},{8,4},{12,8},{16,12},{20,16},{24,20},{28,24},{1,29},{... | collective-permute-start | bytes 1179656 | tf_op jit(solution)/shard_map/ppermute | solution.py:26
  41.6 11.9 %collective-permute-start.16 = (f32[2,6,64,128]{3,2,1,0:T(8,128)S(1)}, f32[2,6,64,128]{3,2,1,0:T(8,128)S(1)}, u32[]{:S(2)}, u32[]{:S(2)}) collective-permute-start(f32[2,6,64,128]{3,2,1,0:T(8,128)S(1)} %collective-permute-done.15), channel_id=1, source_target_pairs={{0,4},{4,8},{8,12},{12,16},{16,20},{20,24},{24,28},{28,0},{1,5},{5... | collective-permute-start | bytes 1179656 | tf_op jit(solution)/shard_map/ppermute | solution.py:26
  46.9 11.9 %collective-permute-start.13 = (f32[2,6,64,128]{3,2,1,0:T(8,128)S(1)}, f32[2,6,64,128]{3,2,1,0:T(8,128)S(1)}, u32[]{:S(2)}, u32[]{:S(2)}) collective-permute-start(f32[2,6,64,128]{3,2,1,0:T(8,128)S(1)} %collective-permute-done.12), channel_id=1, source_target_pairs={{0,28},{4,0},{8,4},{12,8},{16,12},{20,16},{24,20},{28,24},{1,29},{... | collective-permute-start | bytes 1179656 | tf_op jit(solution)/shard_map/ppermute | solution.py:26
  50.6 25.3 %collective-permute-start.26 = (f32[2,6,64,128]{3,2,1,0:T(8,128)S(1)}, f32[2,6,64,128]{3,2,1,0:T(8,128)S(1)}, u32[]{:S(2)}, u32[]{:S(2)}) collective-permute-start(f32[2,6,64,128]{3,2,1,0:T(8,128)S(1)} %collective-permute-done.15), channel_id=1, source_target_pairs={{0,1},{1,0},{2,3},{3,2},{4,5},{5,4},{6,7},{7,6},{8,9},{9,8},{10,11... | collective-permute-start | bytes 1179656 | tf_op jit(solution)/shard_map/ppermute | solution.py:21
  53.5 11.0 %collective-permute-start.17 = (f32[2,6,64,128]{3,2,1,0:T(8,128)S(1)}, f32[2,6,64,128]{3,2,1,0:T(8,128)S(1)}, u32[]{:S(2)}, u32[]{:S(2)}) collective-permute-start(f32[2,6,64,128]{3,2,1,0:T(8,128)S(1)} %collective-permute-done.16), channel_id=1, source_target_pairs={{0,4},{4,8},{8,12},{12,16},{16,20},{20,24},{24,28},{28,0},{1,5},{5... | collective-permute-start | bytes 1179656 | tf_op jit(solution)/shard_map/ppermute | solution.py:26
  58.8 5.8 %collective-permute-start.21 = (f32[2,6,64,128]{3,2,1,0:T(8,128)S(1)}, f32[2,6,64,128]{3,2,1,0:T(8,128)S(1)}, u32[]{:S(2)}, u32[]{:S(2)}) collective-permute-start(f32[2,6,64,128]{3,2,1,0:T(8,128)S(1)} %collective-permute-done.12), channel_id=1, source_target_pairs={{0,1},{1,0},{2,3},{3,2},{4,5},{5,4},{6,7},{7,6},{8,9},{9,8},{10,11... | collective-permute-start | bytes 1179656 | tf_op jit(solution)/shard_map/ppermute | solution.py:21
  64.5 11.4 %collective-permute-start.25 = (f32[2,6,64,128]{3,2,1,0:T(8,128)S(1)}, f32[2,6,64,128]{3,2,1,0:T(8,128)S(1)}, u32[]{:S(2)}, u32[]{:S(2)}) collective-permute-start(f32[2,6,64,128]{3,2,1,0:T(8,128)S(1)} %collective-permute-done.16), channel_id=1, source_target_pairs={{0,1},{1,0},{2,3},{3,2},{4,5},{5,4},{6,7},{7,6},{8,9},{9,8},{10,11... | collective-permute-start | bytes 1179656 | tf_op jit(solution)/shard_map/ppermute | solution.py:21
  64.5 7.4 %collective-permute-start.14 = (f32[6,64,128]{2,1,0:T(8,128)S(1)}, f32[6,64,128]{2,1,0:T(8,128)S(1)}, u32[]{:S(2)}, u32[]{:S(2)}) collective-permute-start(f32[6,64,128]{2,1,0:T(8,128)S(1)} %slice_bitcast_fusion.3), channel_id=1, source_target_pairs={{0,28},{4,0},{8,4},{12,8},{16,12},{20,16},{24,20},{28,24},{1,29},{... | collective-permute-start | bytes 589832 | tf_op jit(solution)/shard_map/ppermute | solution.py:26
  64.7 8.6 %collective-permute-start.18 = (f32[6,64,128]{2,1,0:T(8,128)S(1)}, f32[6,64,128]{2,1,0:T(8,128)S(1)}, u32[]{:S(2)}, u32[]{:S(2)}) collective-permute-start(f32[6,64,128]{2,1,0:T(8,128)S(1)} %slice_bitcast_fusion.2), channel_id=1, source_target_pairs={{0,4},{4,8},{8,12},{12,16},{16,20},{20,24},{24,28},{28,0},{1,5},{5... | collective-permute-start | bytes 589832 | tf_op jit(solution)/shard_map/ppermute | solution.py:26
  66.8 6.7 %collective-permute-start.22 = (f32[2,6,64,128]{3,2,1,0:T(8,128)S(1)}, f32[2,6,64,128]{3,2,1,0:T(8,128)S(1)}, u32[]{:S(2)}, u32[]{:S(2)}) collective-permute-start(f32[2,6,64,128]{3,2,1,0:T(8,128)S(1)} %collective-permute-done.13), channel_id=1, source_target_pairs={{0,1},{1,0},{2,3},{3,2},{4,5},{5,4},{6,7},{7,6},{8,9},{9,8},{10,11... | collective-permute-start | bytes 1179656 | tf_op jit(solution)/shard_map/ppermute | solution.py:21
  73.6 14.4 %collective-permute-start.8 = (f32[16,64,128]{2,1,0:T(8,128)S(1)}, f32[16,64,128]{2,1,0:T(8,128)S(1)}, u32[]{:S(2)}, u32[]{:S(2)}) collective-permute-start(f32[16,64,128]{2,1,0:T(8,128)S(1)} %slice_bitcast_fusion.1), channel_id=1, source_target_pairs={{0,96},{32,0},{64,32},{96,64},{1,97},{33,1},{65,33},{97,65},{2,98}... | collective-permute-start | bytes 1572872 | tf_op jit(solution)/shard_map/ppermute | solution.py:26
  75.1 15.2 %collective-permute-start.9 = (f32[16,64,128]{2,1,0:T(8,128)S(1)}, f32[16,64,128]{2,1,0:T(8,128)S(1)}, u32[]{:S(2)}, u32[]{:S(2)}) collective-permute-start(f32[16,64,128]{2,1,0:T(8,128)S(1)} %slice_bitcast_fusion), channel_id=1, source_target_pairs={{0,32},{32,64},{64,96},{96,0},{1,33},{33,65},{65,97},{97,1},{2,34}... | collective-permute-start | bytes 1572872 | tf_op jit(solution)/shard_map/ppermute | solution.py:26
  (8 other events, 75.0 us)
where the time goes:
time: 105 us
  waiting for transfers between devices  54.5 us (52%)
  starting transfers between devices  29.7 us (28%)
  Pallas kernels  14.5 us (14%)
  local copies, waits for them, and re-layouts  4.71 us (4%)
  other arithmetic  1.08 us (1%)
    ppermute x16, waiting for transfers between devices, shift(): lax.ppermute(block, axis, [(i, (i + distance) % n) for i in range(n)])  53 us
    ppermute x16, starting transfers between devices, shift(): lax.ppermute(block, axis, [(i, (i + distance) % n) for i in range(n)])  24.5 us
    pallas_call x1, Pallas kernels, product(): pl.pallas_call(functools.partial(product_kernel, len(pieces)), out_shape=...  14.5 us
    ppermute x11, starting transfers between devices, swap(): return lax.ppermute(block, axis, [(0, 1), (1, 0)])  5.13 us
    another operation x2, local copies, waits for them, and re-layouts, as_pairs(): blocks = panel.reshape(slots // 2, 2, BLK, BLK)  2.26 us
  transfers between devices with their start and end apart: 27, of which 14 were waited for; matrix products, arithmetic and copies ran while one was open for 5% of the time, Pallas kernels for 0%

commit v1 on v0

--- a/solution.py
+++ b/solution.py
@@ -60,8 +60,7 @@
     far_down = shift(down[1], "z", 1)
     by_offset[half] = jnp.stack([far_up, far_down])
     mine = jnp.stack(by_offset)
-    other = jnp.stack([swap(piece, "core") for piece in by_offset])
-    return mine, other
+    return mine, swap(mine, "core")
 
 
 def product_kernel(n_pieces, index_ref, rows_ref, *refs):
@@ -81,23 +80,33 @@
                 pair = a_ref[j, t]
                 pair_hi = pair.astype(jnp.bfloat16)
                 pair_lo = (pair - pair_hi.astype(jnp.float32)).astype(jnp.bfloat16)
+                both = jnp.concatenate([pair_hi, pair_lo], axis=0)
+                rows_a = pair.shape[0]
+                targets = []
+                halves_hi = []
+                halves_lo = []
                 for u in range(2):
                     g = base + 2 * t + u
-                    row = jnp.minimum(rows_ref[g], blocks)
+                    targets.append(jnp.minimum(rows_ref[g], blocks))
                     index = index_ref[g]
                     local = index % stripes
                     right = jnp.where(index < stripes, mine_ref[local], other_ref[local])
                     right_hi = right.astype(jnp.bfloat16)
                     right_lo = (right - right_hi.astype(jnp.float32)).astype(jnp.bfloat16)
                     zeros = jnp.zeros_like(right_hi)
-                    pieces_hi = [right_hi, zeros] if u == 0 else [zeros, right_hi]
-                    pieces_lo = [right_lo, zeros] if u == 0 else [zeros, right_lo]
-                    right_hi = jnp.concatenate(pieces_hi, axis=0)
-                    right_lo = jnp.concatenate(pieces_lo, axis=0)
-                    term = jnp.dot(pair_hi, right_hi, preferred_element_type=jnp.float32)
-                    term += jnp.dot(pair_hi, right_lo, preferred_element_type=jnp.float32)
-                    term += jnp.dot(pair_lo, right_hi, preferred_element_type=jnp.float32)
-                    acc_ref[row] += term
+                    halves_hi.append(jnp.concatenate([right_hi, zeros] if u == 0 else [zeros, right_hi], axis=0))
+                    halves_lo.append(jnp.concatenate([right_lo, zeros] if u == 0 else [zeros, right_lo], axis=0))
+                diag_hi = jnp.concatenate(halves_hi, axis=1)
+                diag_lo = jnp.concatenate(halves_lo, axis=1)
+                with_hi = jnp.dot(both, diag_hi, preferred_element_type=jnp.float32)
+                with_lo = jnp.dot(pair_hi, diag_lo, preferred_element_type=jnp.float32)
+                columns = mine_ref.shape[2]
+                for u in range(2):
+                    cols = slice(u * columns, (u + 1) * columns)
+                    term = with_hi[:rows_a, cols]
+                    term += with_lo[:, cols]
+                    term += with_hi[rows_a:, cols]
+                    acc_ref[targets[u]] += term
                 return carry
 
             lax.fori_loop(0, n_pairs, one_pair, 0, unroll=4)

time: 105 us -> 132 us (1.26)
  waiting for transfers between devices: 54.5 us -> 72.9 us
  local copies, waits for them, and re-layouts: 4.71 us -> 9.52 us
  starting transfers between devices: 29.7 us -> 32.6 us
  other arithmetic: 1.08 us -> 3.69 us
    ppermute x11 -> x4, waiting for transfers between devices: 1.44 us -> 17.6 us  [swap(): return lax.ppermute(block, axis, [(0, 1), (1, 0)])]
    ppermute x16, starting transfers between devices: 24.5 us -> 28.3 us  [shift(): lax.ppermute(block, axis, [(i, (i + distance) % n) for i in range(n)])]
    unnamed x26 -> x15, local copies, waits for them, and re-layouts: 0.39 us -> 3.96 us
    unnamed x3, other arithmetic: 0.06 us -> 2.51 us
    ppermute x16, waiting for transfers between devices: 53 us -> 55.2 us  [shift(): lax.ppermute(block, axis, [(i, (i + distance) % n) for i in range(n)])]
    ppermute x11 -> x4, starting transfers between devices: 5.13 us -> 4.33 us  [swap(): return lax.ppermute(block, axis, [(0, 1), (1, 0)])]
  transfers between devices with their start and end apart: 27 -> 20, of which waited for: 14 -> 11; matrix products, arithmetic and copies ran while one was open for 5% -> 7% of each run, Pallas kernels for 0% -> 0%
where the time goes in v1:
time: 132 us
  waiting for transfers between devices  72.9 us (55%)
  starting transfers between devices  32.6 us (25%)
  Pallas kernels  13.3 us (10%)
  local copies, waits for them, and re-layouts  9.52 us (7%)
  other arithmetic  3.69 us (3%)
    ppermute x16, waiting for transfers between devices, shift(): lax.ppermute(block, axis, [(i, (i + distance) % n) for i in range(n)])  55.2 us
    ppermute x16, starting transfers between devices, shift(): lax.ppermute(block, axis, [(i, (i + distance) % n) for i in range(n)])  28.3 us
    ppermute x4, waiting for transfers between devices, swap(): return lax.ppermute(block, axis, [(0, 1), (1, 0)])  17.6 us
    pallas_call x1, Pallas kernels, product(): pl.pallas_call(functools.partial(product_kernel, len(pieces)), out_shape=...  13.3 us
    ppermute x4, starting transfers between devices, swap(): return lax.ppermute(block, axis, [(0, 1), (1, 0)])  4.33 us
    unnamed x15, local copies, waits for them, and re-layouts  3.96 us
  transfers between devices with their start and end apart: 20, of which 11 were waited for; matrix products, arithmetic and copies ran while one was open for 7% of the time, Pallas kernels for 0%

profile of v1, /device:TPU:2, one launch (start us, length us, event | category | flops | bytes accessed | tf_op | source)
XLA Modules:
  0.0 132.1 jit_solution(2230929006763774335)
XLA Ops:
  0.0 2.1 %collective-permute-start.10 = (f32[6,64,128]{2,1,0:T(8,128)}, f32[6,64,128]{2,1,0:T(8,128)S(1)}, u32[]{:S(2)}, u32[]{:S(2)}) collective-permute-start(f32[6,64,128]{2,1,0:T(8,128)} %param.7), channel_id=1, source_target_pairs={{0,2},{2,0},{1,3},{3,1},{4,6},{6,4},{5,7},{7,5},{8,10},{10,8},{9,1... | collective-permute-start | bytes 589832 | tf_op jit(solution)/shard_map/ppermute | solution.py:21
  2.1 6.2 %collective-permute-done.10 = f32[6,64,128]{2,1,0:T(8,128)S(1)} collective-permute-done((f32[6,64,128]{2,1,0:T(8,128)}, f32[6,64,128]{2,1,0:T(8,128)S(1)}, u32[]{:S(2)}, u32[]{:S(2)}) %collective-permute-start.10) | collective-permute-done | bytes 196640 | tf_op jit(solution)/shard_map/ppermute | solution.py:21
  8.4 1.0 pad_maximum_fusion.1
  9.3 5.9 %collective-permute-start.11 = (f32[2,6,64,128]{3,2,1,0:T(8,128)S(1)}, f32[2,6,64,128]{3,2,1,0:T(8,128)S(1)}, u32[]{:S(2)}, u32[]{:S(2)}) collective-permute-start(f32[2,6,64,128]{3,2,1,0:T(8,128)S(1)} %pad_maximum_fusion.1), channel_id=1, source_target_pairs={{0,28},{4,0},{8,4},{12,8},{16,12},{20,16},{24,20},{28,24},{1,29},{... | collective-permute-start | bytes 1179656 | tf_op jit(solution)/shard_map/ppermute | solution.py:26
  15.2 7.5 %collective-permute-done.11 = f32[2,6,64,128]{3,2,1,0:T(8,128)S(1)} collective-permute-done((f32[2,6,64,128]{3,2,1,0:T(8,128)S(1)}, f32[2,6,64,128]{3,2,1,0:T(8,128)S(1)}, u32[]{:S(2)}, u32[]{:S(2)}) %collective-permute-start.11) | collective-permute-done | bytes 393248 | tf_op jit(solution)/shard_map/ppermute | solution.py:26
  22.8 3.7 %collective-permute-start.12 = (f32[2,6,64,128]{3,2,1,0:T(8,128)S(1)}, f32[2,6,64,128]{3,2,1,0:T(8,128)S(1)}, u32[]{:S(2)}, u32[]{:S(2)}) collective-permute-start(f32[2,6,64,128]{3,2,1,0:T(8,128)S(1)} %collective-permute-done.11), channel_id=1, source_target_pairs={{0,28},{4,0},{8,4},{12,8},{16,12},{20,16},{24,20},{28,24},{1,29},{... | collective-permute-start | bytes 1179656 | tf_op jit(solution)/shard_map/ppermute | solution.py:26
  26.5 1.7 %bitcast_dynamic-update-slice_fusion.6 = f32[8,2,6,64,128]{4,3,2,1,0:T(8,128)} fusion(f32[1,6,64,128]{3,2,1,0:T(8,128)S(1)} %bitcast.71, f32[1,6,64,128]{3,2,1,0:T(8,128)} %bitcast.69), kind=kLoop, calls=%fused_computation.13 | loop fusion | flops 98303 | bytes 786432
  28.2 5.0 %collective-permute-done.12 = f32[2,6,64,128]{3,2,1,0:T(8,128)S(1)} collective-permute-done((f32[2,6,64,128]{3,2,1,0:T(8,128)S(1)}, f32[2,6,64,128]{3,2,1,0:T(8,128)S(1)}, u32[]{:S(2)}, u32[]{:S(2)}) %collective-permute-start.12) | collective-permute-done | bytes 393248 | tf_op jit(solution)/shard_map/ppermute | solution.py:26
  33.1 3.7 %collective-permute-start.13 = (f32[2,6,64,128]{3,2,1,0:T(8,128)S(1)}, f32[2,6,64,128]{3,2,1,0:T(8,128)S(1)}, u32[]{:S(2)}, u32[]{:S(2)}) collective-permute-start(f32[2,6,64,128]{3,2,1,0:T(8,128)S(1)} %collective-permute-done.12), channel_id=1, source_target_pairs={{0,28},{4,0},{8,4},{12,8},{16,12},{20,16},{24,20},{28,24},{1,29},{... | collective-permute-start | bytes 1179656 | tf_op jit(solution)/shard_map/ppermute | solution.py:26
  38.4 4.3 %collective-permute-done.13 = f32[2,6,64,128]{3,2,1,0:T(8,128)S(1)} collective-permute-done((f32[2,6,64,128]{3,2,1,0:T(8,128)S(1)}, f32[2,6,64,128]{3,2,1,0:T(8,128)S(1)}, u32[]{:S(2)}, u32[]{:S(2)}) %collective-permute-start.13) | collective-permute-done | bytes 393248 | tf_op jit(solution)/shard_map/ppermute | solution.py:26
  42.6 3.8 %collective-permute-start.14 = (f32[6,64,128]{2,1,0:T(8,128)S(1)}, f32[6,64,128]{2,1,0:T(8,128)S(1)}, u32[]{:S(2)}, u32[]{:S(2)}) collective-permute-start(f32[6,64,128]{2,1,0:T(8,128)S(1)} %slice_bitcast_fusion.3), channel_id=1, source_target_pairs={{0,28},{4,0},{8,4},{12,8},{16,12},{20,16},{24,20},{28,24},{1,29},{... | collective-permute-start | bytes 589832 | tf_op jit(solution)/shard_map/ppermute | solution.py:26
  47.7 1.9 %collective-permute-done.14 = f32[6,64,128]{2,1,0:T(8,128)S(1)} collective-permute-done((f32[6,64,128]{2,1,0:T(8,128)S(1)}, f32[6,64,128]{2,1,0:T(8,128)S(1)}, u32[]{:S(2)}, u32[]{:S(2)}) %collective-permute-start.14) | collective-permute-done | bytes 196640 | tf_op jit(solution)/shard_map/ppermute | solution.py:26
  49.6 4.2 %collective-permute-done.18 = f32[6,64,128]{2,1,0:T(8,128)S(1)} collective-permute-done((f32[6,64,128]{2,1,0:T(8,128)S(1)}, f32[6,64,128]{2,1,0:T(8,128)S(1)}, u32[]{:S(2)}, u32[]{:S(2)}) %collective-permute-start.18) | collective-permute-done | bytes 196640 | tf_op jit(solution)/shard_map/ppermute | solution.py:26
  59.4 1.6 %collective-permute-start = (s32[2,32]{1,0:T(2,128)S(1)}, s32[2,32]{1,0:T(2,128)S(1)}, u32[]{:S(2)}, u32[]{:S(2)}) collective-permute-start(s32[2,32]{1,0:T(2,128)S(1)} %get-tuple-element.12), channel_id=1, source_target_pairs={{0,128},{128,0},{1,129},{129,1},{2,130},{130,2},{3,131},{131,3},{4... | collective-permute-start | bytes 776 | tf_op jit(solution)/shard_map/ppermute | solution.py:21
  61.8 11.4 %collective-permute-done = s32[2,32]{1,0:T(2,128)S(1)} collective-permute-done((s32[2,32]{1,0:T(2,128)S(1)}, s32[2,32]{1,0:T(2,128)S(1)}, u32[]{:S(2)}, u32[]{:S(2)}) %collective-permute-start) | collective-permute-done | bytes 288 | tf_op jit(solution)/shard_map/ppermute | solution.py:21
  73.3 1.6 %collective-permute-start.1 = (s32[2,2,32]{2,1,0:T(2,128)S(1)}, s32[2,2,32]{2,1,0:T(2,128)S(1)}, u32[]{:S(2)}, u32[]{:S(2)}) collective-permute-start(s32[2,2,32]{2,1,0:T(2,128)S(1)} %pad_add_fusion), channel_id=1, source_target_pairs={{0,32},{32,64},{64,96},{96,0},{1,33},{33,65},{65,97},{97,1},{2,34}... | collective-permute-start | bytes 1544 | tf_op jit(solution)/shard_map/ppermute | solution.py:26
  74.8 1.7 %collective-permute-start.2 = (s32[2,2,32]{2,1,0:T(2,128)S(1)}, s32[2,2,32]{2,1,0:T(2,128)S(1)}, u32[]{:S(2)}, u32[]{:S(2)}) collective-permute-start(s32[2,2,32]{2,1,0:T(2,128)S(1)} %pad_add_fusion), channel_id=1, source_target_pairs={{0,96},{32,0},{64,32},{96,64},{1,97},{33,1},{65,33},{97,65},{2,98}... | collective-permute-start | bytes 1544 | tf_op jit(solution)/shard_map/ppermute | solution.py:26
  76.6 1.8 %collective-permute-start.7 = (f32[2,16,64,128]{3,2,1,0:T(8,128)S(1)}, f32[2,16,64,128]{3,2,1,0:T(8,128)S(1)}, u32[]{:S(2)}, u32[]{:S(2)}) collective-permute-start(f32[2,16,64,128]{3,2,1,0:T(8,128)S(1)} %pad_maximum_fusion), channel_id=1, source_target_pairs={{0,96},{32,0},{64,32},{96,64},{1,97},{33,1},{65,33},{97,65},{2,98}... | collective-permute-start | bytes 3145736 | tf_op jit(solution)/shard_map/ppermute | solution.py:26
  78.7 3.0 %collective-permute-start.3 = (s32[2,32]{1,0:T(2,128)S(1)}, s32[2,32]{1,0:T(2,128)S(1)}, u32[]{:S(2)}, u32[]{:S(2)}) collective-permute-start(s32[2,32]{1,0:T(2,128)S(1)} %slice_bitcast_fusion.5), channel_id=1, source_target_pairs={{0,96},{32,0},{64,32},{96,64},{1,97},{33,1},{65,33},{97,65},{2,98}... | collective-permute-start | bytes 776 | tf_op jit(solution)/shard_map/ppermute | solution.py:26
  81.7 19.4 %collective-permute-done.3 = s32[2,32]{1,0:T(2,128)S(1)} collective-permute-done((s32[2,32]{1,0:T(2,128)S(1)}, s32[2,32]{1,0:T(2,128)S(1)}, u32[]{:S(2)}, u32[]{:S(2)}) %collective-permute-start.3) | collective-permute-done | bytes 288 | tf_op jit(solution)/shard_map/ppermute | solution.py:26
  102.0 2.7 %collective-permute-start.8 = (f32[16,64,128]{2,1,0:T(8,128)}, f32[16,64,128]{2,1,0:T(8,128)}, u32[]{:S(2)}, u32[]{:S(2)}) collective-permute-start(f32[16,64,128]{2,1,0:T(8,128)} %slice_bitcast_fusion.1), channel_id=1, source_target_pairs={{0,96},{32,0},{64,32},{96,64},{1,97},{33,1},{65,33},{97,65},{2,98}... | collective-permute-start | bytes 1572872 | tf_op jit(solution)/shard_map/ppermute | solution.py:26
  106.2 8.4 %collective-permute-done.8 = f32[16,64,128]{2,1,0:T(8,128)} collective-permute-done((f32[16,64,128]{2,1,0:T(8,128)}, f32[16,64,128]{2,1,0:T(8,128)}, u32[]{:S(2)}, u32[]{:S(2)}) %collective-permute-start.8) | collective-permute-done | bytes 524320 | tf_op jit(solution)/shard_map/ppermute | solution.py:26
  114.6 4.2 %collective-permute-done.9 = f32[16,64,128]{2,1,0:T(8,128)} collective-permute-done((f32[16,64,128]{2,1,0:T(8,128)}, f32[16,64,128]{2,1,0:T(8,128)}, u32[]{:S(2)}, u32[]{:S(2)}) %collective-permute-start.9) | collective-permute-done | bytes 524320 | tf_op jit(solution)/shard_map/ppermute | solution.py:26
  118.8 13.3 %shard_map.46 = f32[32,64,128]{2,1,0:T(8,128)} custom-call(s32[256]{0:T(256)S(1)} %fusion.6.index_ref, s32[256]{0:T(256)S(1)} %reshape_squeeze.6.rows_ref, f32[1,16,64,128]{3,2,1,0:T(8,128)S(1)} %broadcast_in_dim_reshape.3.refs_0_, f32[1,16,64,128]{3,2,1,0:T(8,128)S(1)} %bitcast.65, f32[2,16,64,128]{3,2,1,0:T(8,128)S(1)} %collective-permute-done.6.refs_2_, ...), custom_call_target="tpu_custom_call" | custom-call | flops 268435456 | bytes 11534336 | tf_op jit(solution)/shard_map/pallas_call | solution.py:123
  (64 shorter events, 12.0 us)
Async XLA Ops:
  0.0 8.4 %collective-permute-start.10 = (f32[6,64,128]{2,1,0:T(8,128)}, f32[6,64,128]{2,1,0:T(8,128)S(1)}, u32[]{:S(2)}, u32[]{:S(2)}) collective-permute-start(f32[6,64,128]{2,1,0:T(8,128)} %param.7), channel_id=1, source_target_pairs={{0,2},{2,0},{1,3},{3,1},{4,6},{6,4},{5,7},{7,5},{8,10},{10,8},{9,1... | collective-permute-start | bytes 589832 | tf_op jit(solution)/shard_map/ppermute | solution.py:21
  9.3 13.5 %collective-permute-start.11 = (f32[2,6,64,128]{3,2,1,0:T(8,128)S(1)}, f32[2,6,64,128]{3,2,1,0:T(8,128)S(1)}, u32[]{:S(2)}, u32[]{:S(2)}) collective-permute-start(f32[2,6,64,128]{3,2,1,0:T(8,128)S(1)} %pad_maximum_fusion.1), channel_id=1, source_target_pairs={{0,28},{4,0},{8,4},{12,8},{16,12},{20,16},{24,20},{28,24},{1,29},{... | collective-permute-start | bytes 1179656 | tf_op jit(solution)/shard_map/ppermute | solution.py:26
  15.2 11.2 %collective-permute-start.15 = (f32[2,6,64,128]{3,2,1,0:T(8,128)S(1)}, f32[2,6,64,128]{3,2,1,0:T(8,128)S(1)}, u32[]{:S(2)}, u32[]{:S(2)}) collective-permute-start(f32[2,6,64,128]{3,2,1,0:T(8,128)S(1)} %pad_maximum_fusion.1), channel_id=1, source_target_pairs={{0,4},{4,8},{8,12},{12,16},{16,20},{20,24},{24,28},{28,0},{1,5},{5... | collective-permute-start | bytes 1179656 | tf_op jit(solution)/shard_map/ppermute | solution.py:26
  22.8 10.4 %collective-permute-start.12 = (f32[2,6,64,128]{3,2,1,0:T(8,128)S(1)}, f32[2,6,64,128]{3,2,1,0:T(8,128)S(1)}, u32[]{:S(2)}, u32[]{:S(2)}) collective-permute-start(f32[2,6,64,128]{3,2,1,0:T(8,128)S(1)} %collective-permute-done.11), channel_id=1, source_target_pairs={{0,28},{4,0},{8,4},{12,8},{16,12},{20,16},{24,20},{28,24},{1,29},{... | collective-permute-start | bytes 1179656 | tf_op jit(solution)/shard_map/ppermute | solution.py:26
  26.5 11.1 %collective-permute-start.16 = (f32[2,6,64,128]{3,2,1,0:T(8,128)S(1)}, f32[2,6,64,128]{3,2,1,0:T(8,128)S(1)}, u32[]{:S(2)}, u32[]{:S(2)}) collective-permute-start(f32[2,6,64,128]{3,2,1,0:T(8,128)S(1)} %collective-permute-done.15), channel_id=1, source_target_pairs={{0,4},{4,8},{8,12},{12,16},{16,20},{20,24},{24,28},{28,0},{1,5},{5... | collective-permute-start | bytes 1179656 | tf_op jit(solution)/shard_map/ppermute | solution.py:26
  28.2 28.8 %copy-start = (f32[1,1,32,4096]{3,2,1,0:T(8,128)S(1)}, f32[1,1,32,4096]{3,2,1,0:T(8,128)}, u32[]{:S(2)}) copy-start(f32[1,1,32,4096]{3,2,1,0:T(8,128)} %param.4) | copy-start | bytes 1572868
  33.1 9.5 %collective-permute-start.13 = (f32[2,6,64,128]{3,2,1,0:T(8,128)S(1)}, f32[2,6,64,128]{3,2,1,0:T(8,128)S(1)}, u32[]{:S(2)}, u32[]{:S(2)}) collective-permute-start(f32[2,6,64,128]{3,2,1,0:T(8,128)S(1)} %collective-permute-done.12), channel_id=1, source_target_pairs={{0,28},{4,0},{8,4},{12,8},{16,12},{20,16},{24,20},{28,24},{1,29},{... | collective-permute-start | bytes 1179656 | tf_op jit(solution)/shard_map/ppermute | solution.py:26
  37.6 9.2 %collective-permute-start.17 = (f32[2,6,64,128]{3,2,1,0:T(8,128)S(1)}, f32[2,6,64,128]{3,2,1,0:T(8,128)S(1)}, u32[]{:S(2)}, u32[]{:S(2)}) collective-permute-start(f32[2,6,64,128]{3,2,1,0:T(8,128)S(1)} %collective-permute-done.16), channel_id=1, source_target_pairs={{0,4},{4,8},{8,12},{12,16},{16,20},{20,24},{24,28},{28,0},{1,5},{5... | collective-permute-start | bytes 1179656 | tf_op jit(solution)/shard_map/ppermute | solution.py:26
  42.6 7.0 %collective-permute-start.14 = (f32[6,64,128]{2,1,0:T(8,128)S(1)}, f32[6,64,128]{2,1,0:T(8,128)S(1)}, u32[]{:S(2)}, u32[]{:S(2)}) collective-permute-start(f32[6,64,128]{2,1,0:T(8,128)S(1)} %slice_bitcast_fusion.3), channel_id=1, source_target_pairs={{0,28},{4,0},{8,4},{12,8},{16,12},{20,16},{24,20},{28,24},{1,29},{... | collective-permute-start | bytes 589832 | tf_op jit(solution)/shard_map/ppermute | solution.py:26
  46.8 7.0 %collective-permute-start.18 = (f32[6,64,128]{2,1,0:T(8,128)S(1)}, f32[6,64,128]{2,1,0:T(8,128)S(1)}, u32[]{:S(2)}, u32[]{:S(2)}) collective-permute-start(f32[6,64,128]{2,1,0:T(8,128)S(1)} %slice_bitcast_fusion.2), channel_id=1, source_target_pairs={{0,4},{4,8},{8,12},{12,16},{16,20},{20,24},{24,28},{28,0},{1,5},{5... | collective-permute-start | bytes 589832 | tf_op jit(solution)/shard_map/ppermute | solution.py:26
  56.2 3.2 %copy-start.1 = (s32[1,1,32]{2,1,0:T(1,128)S(1)}, s32[1,1,32]{2,1,0:T(1,128)}, u32[]{:S(2)}) copy-start(s32[1,1,32]{2,1,0:T(1,128)} %param.6) | copy-start | bytes 388
  56.2 3.2 %copy-start.2 = (s32[1,1,32]{2,1,0:T(1,128)S(1)}, s32[1,1,32]{2,1,0:T(1,128)}, u32[]{:S(2)}) copy-start(s32[1,1,32]{2,1,0:T(1,128)} %param.5) | copy-start | bytes 388
  56.9 61.8 %collective-permute-start.19 = (f32[8,2,6,64,128]{4,3,2,1,0:T(8,128)}, f32[8,2,6,64,128]{4,3,2,1,0:T(8,128)}, u32[]{:S(2)}, u32[]{:S(2)}) collective-permute-start(f32[8,2,6,64,128]{4,3,2,1,0:T(8,128)} %bitcast_dynamic-update-slice_fusion), channel_id=1, source_target_pairs={{0,1},{1,0},{2,3},{3,2},{4,5},{5,4},{6,7},{7,6},{8,9},{9,8},{10,11... | collective-permute-start | bytes 9437192 | tf_op jit(solution)/shard_map/ppermute | solution.py:21
  58.8 17.8 %collective-permute-start.5 = (f32[16,64,128]{2,1,0:T(8,128)S(1)}, f32[16,64,128]{2,1,0:T(8,128)S(1)}, u32[]{:S(2)}, u32[]{:S(2)}) collective-permute-start(f32[16,64,128]{2,1,0:T(8,128)S(1)} %reshape.111), channel_id=1, source_target_pairs={{0,128},{128,0},{1,129},{129,1},{2,130},{130,2},{3,131},{131,3},{4... | collective-permute-start | bytes 1572872 | tf_op jit(solution)/shard_map/ppermute | solution.py:21
  59.4 13.8 %collective-permute-start = (s32[2,32]{1,0:T(2,128)S(1)}, s32[2,32]{1,0:T(2,128)S(1)}, u32[]{:S(2)}, u32[]{:S(2)}) collective-permute-start(s32[2,32]{1,0:T(2,128)S(1)} %get-tuple-element.12), channel_id=1, source_target_pairs={{0,128},{128,0},{1,129},{129,1},{2,130},{130,2},{3,131},{131,3},{4... | collective-permute-start | bytes 776 | tf_op jit(solution)/shard_map/ppermute | solution.py:21
  73.3 8.4 %collective-permute-start.1 = (s32[2,2,32]{2,1,0:T(2,128)S(1)}, s32[2,2,32]{2,1,0:T(2,128)S(1)}, u32[]{:S(2)}, u32[]{:S(2)}) collective-permute-start(s32[2,2,32]{2,1,0:T(2,128)S(1)} %pad_add_fusion), channel_id=1, source_target_pairs={{0,32},{32,64},{64,96},{96,0},{1,33},{33,65},{65,97},{97,1},{2,34}... | collective-permute-start | bytes 1544 | tf_op jit(solution)/shard_map/ppermute | solution.py:26
  74.8 3.9 %collective-permute-start.2 = (s32[2,2,32]{2,1,0:T(2,128)S(1)}, s32[2,2,32]{2,1,0:T(2,128)S(1)}, u32[]{:S(2)}, u32[]{:S(2)}) collective-permute-start(s32[2,2,32]{2,1,0:T(2,128)S(1)} %pad_add_fusion), channel_id=1, source_target_pairs={{0,96},{32,0},{64,32},{96,64},{1,97},{33,1},{65,33},{97,65},{2,98}... | collective-permute-start | bytes 1544 | tf_op jit(solution)/shard_map/ppermute | solution.py:26
  76.6 24.5 %collective-permute-start.7 = (f32[2,16,64,128]{3,2,1,0:T(8,128)S(1)}, f32[2,16,64,128]{3,2,1,0:T(8,128)S(1)}, u32[]{:S(2)}, u32[]{:S(2)}) collective-permute-start(f32[2,16,64,128]{3,2,1,0:T(8,128)S(1)} %pad_maximum_fusion), channel_id=1, source_target_pairs={{0,96},{32,0},{64,32},{96,64},{1,97},{33,1},{65,33},{97,65},{2,98}... | collective-permute-start | bytes 3145736 | tf_op jit(solution)/shard_map/ppermute | solution.py:26
  78.5 26.2 %collective-permute-start.6 = (f32[2,16,64,128]{3,2,1,0:T(8,128)S(1)}, f32[2,16,64,128]{3,2,1,0:T(8,128)S(1)}, u32[]{:S(2)}, u32[]{:S(2)}) collective-permute-start(f32[2,16,64,128]{3,2,1,0:T(8,128)S(1)} %pad_maximum_fusion), channel_id=1, source_target_pairs={{0,32},{32,64},{64,96},{96,0},{1,33},{33,65},{65,97},{97,1},{2,34}... | collective-permute-start | bytes 3145736 | tf_op jit(solution)/shard_map/ppermute | solution.py:26
  78.7 22.4 %collective-permute-start.3 = (s32[2,32]{1,0:T(2,128)S(1)}, s32[2,32]{1,0:T(2,128)S(1)}, u32[]{:S(2)}, u32[]{:S(2)}) collective-permute-start(s32[2,32]{1,0:T(2,128)S(1)} %slice_bitcast_fusion.5), channel_id=1, source_target_pairs={{0,96},{32,0},{64,32},{96,64},{1,97},{33,1},{65,33},{97,65},{2,98}... | collective-permute-start | bytes 776 | tf_op jit(solution)/shard_map/ppermute | solution.py:26
  81.7 23.8 %collective-permute-start.4 = (s32[2,32]{1,0:T(2,128)S(1)}, s32[2,32]{1,0:T(2,128)S(1)}, u32[]{:S(2)}, u32[]{:S(2)}) collective-permute-start(s32[2,32]{1,0:T(2,128)S(1)} %slice_bitcast_fusion.4), channel_id=1, source_target_pairs={{0,32},{32,64},{64,96},{96,0},{1,33},{33,65},{65,97},{97,1},{2,34}... | collective-permute-start | bytes 776 | tf_op jit(solution)/shard_map/ppermute | solution.py:26
  102.0 12.6 %collective-permute-start.8 = (f32[16,64,128]{2,1,0:T(8,128)}, f32[16,64,128]{2,1,0:T(8,128)}, u32[]{:S(2)}, u32[]{:S(2)}) collective-permute-start(f32[16,64,128]{2,1,0:T(8,128)} %slice_bitcast_fusion.1), channel_id=1, source_target_pairs={{0,96},{32,0},{64,32},{96,64},{1,97},{33,1},{65,33},{97,65},{2,98}... | collective-permute-start | bytes 1572872 | tf_op jit(solution)/shard_map/ppermute | solution.py:26
  105.5 13.2 %collective-permute-start.9 = (f32[16,64,128]{2,1,0:T(8,128)}, f32[16,64,128]{2,1,0:T(8,128)}, u32[]{:S(2)}, u32[]{:S(2)}) collective-permute-start(f32[16,64,128]{2,1,0:T(8,128)} %slice_bitcast_fusion), channel_id=1, source_target_pairs={{0,32},{32,64},{64,96},{96,0},{1,33},{33,65},{65,97},{97,1},{2,34}... | collective-permute-start | bytes 1572872 | tf_op jit(solution)/shard_map/ppermute | solution.py:26

commit v2 on v0

--- a/solution.py
+++ b/solution.py
@@ -60,13 +60,13 @@
     far_down = shift(down[1], "z", 1)
     by_offset[half] = jnp.stack([far_up, far_down])
     mine = jnp.stack(by_offset)
-    other = jnp.stack([swap(piece, "core") for piece in by_offset])
-    return mine, other
+    early = jnp.stack(by_offset[:half] + by_offset[half + 1:])
+    return mine, swap(early, "core"), swap(by_offset[half], "core")
 
 
 def product_kernel(n_pieces, index_ref, rows_ref, *refs):
     a_refs = refs[:n_pieces]
-    mine_ref, other_ref, out_ref, acc_ref = refs[n_pieces:]
+    mine_ref, early_ref, late_ref, out_ref, acc_ref = refs[n_pieces:]
     acc_ref[...] = jnp.zeros_like(acc_ref)
     blocks = out_ref.shape[0]
     stripes = mine_ref.shape[0]
@@ -81,12 +81,21 @@
                 pair = a_ref[j, t]
                 pair_hi = pair.astype(jnp.bfloat16)
                 pair_lo = (pair - pair_hi.astype(jnp.float32)).astype(jnp.bfloat16)
+                both = jnp.concatenate([pair_hi, pair_lo], axis=0)
+                rows_a = pair.shape[0]
                 for u in range(2):
                     g = base + 2 * t + u
                     row = jnp.minimum(rows_ref[g], blocks)
                     index = index_ref[g]
-                    local = index % stripes
-                    right = jnp.where(index < stripes, mine_ref[local], other_ref[local])
+                    n_early = early_ref.shape[0]
+                    first = jnp.minimum(index, stripes - 1)
+                    second = jnp.clip(index - stripes, 0, n_early - 1)
+                    third = jnp.clip(index - stripes - n_early, 0, late_ref.shape[0] - 1)
+                    right = jnp.where(
+                        index < stripes,
+                        mine_ref[first],
+                        jnp.where(index < stripes + n_early, early_ref[second], late_ref[third]),
+                    )
                     right_hi = right.astype(jnp.bfloat16)
                     right_lo = (right - right_hi.astype(jnp.float32)).astype(jnp.bfloat16)
                     zeros = jnp.zeros_like(right_hi)
@@ -94,9 +103,10 @@
                     pieces_lo = [right_lo, zeros] if u == 0 else [zeros, right_lo]
                     right_hi = jnp.concatenate(pieces_hi, axis=0)
                     right_lo = jnp.concatenate(pieces_lo, axis=0)
-                    term = jnp.dot(pair_hi, right_hi, preferred_element_type=jnp.float32)
+                    with_hi = jnp.dot(both, right_hi, preferred_element_type=jnp.float32)
+                    term = with_hi[:rows_a]
                     term += jnp.dot(pair_hi, right_lo, preferred_element_type=jnp.float32)
-                    term += jnp.dot(pair_lo, right_hi, preferred_element_type=jnp.float32)
+                    term += with_hi[rows_a:]
                     acc_ref[row] += term
                 return carry
 
@@ -105,7 +115,7 @@
     out_ref[...] = acc_ref[:blocks]
 
 
-def product(index, rows, pieces, mine, other):
+def product(index, rows, pieces, mine, early, late):
     _, n_pairs, blk, _ = pieces[0].shape
     n_panels = sum(piece.shape[0] for piece in pieces)
     columns = mine.shape[2]
@@ -114,16 +124,16 @@
     return pl.pallas_call(
         functools.partial(product_kernel, len(pieces)),
         out_shape=jax.ShapeDtypeStruct((MB, blk, columns), jnp.float32),
-        in_specs=[smem, smem] + [vmem] * (len(pieces) + 2),
+        in_specs=[smem, smem] + [vmem] * (len(pieces) + 3),
         out_specs=vmem,
         scratch_shapes=[pltpu.VMEM((MB + 1, blk, columns), jnp.float32)],
         compiler_params=pltpu.CompilerParams(vmem_limit_bytes=48 * 1024 * 1024),
         cost_estimate=pl.CostEstimate(
             flops=2 * 2 * n_panels * n_pairs * blk * blk * columns,
-            bytes_accessed=4 * (sum(piece.size for piece in pieces) + 2 * mine.size + MB * blk * columns),
+            bytes_accessed=4 * (sum(piece.size for piece in pieces) + mine.size + early.size + late.size + MB * blk * columns),
             transcendentals=0,
         ),
-    )(index, rows, *pieces, mine, other)
+    )(index, rows, *pieces, mine, early, late)
 
 
 def as_pairs(panel):
@@ -141,17 +151,20 @@
     ints_k, _ = gather_a(ints)
     ints_k = jnp.concatenate(ints_k)
     a_pieces, pid = gather_a(as_pairs(a_blocks[0, 0]))
-    mine, other = gather_b(b_stripes)
+    mine, early, late = gather_b(b_stripes)
     mine = mine.reshape(-1, BLK, columns)
-    other = other.reshape(-1, BLK, columns)
+    early = early.reshape(-1, BLK, columns)
+    late = late.reshape(-1, BLK, columns)
 
     rows = ints_k[:, 0]
     slots = ints_k[:, 1]
     d = (pid[:, None] - z) % n_z
     core_rel = (slots // 6) % 2 ^ lax.axis_index("core")
     xh_rel = (slots // 12) ^ lax.axis_index("xh")
-    index = ((core_rel * n_z + d) * 2 + xh_rel) * 6 + slots % 6
-    out = product(index.reshape(-1), rows.reshape(-1), a_pieces, mine, other)
+    half = n_z // 2
+    d_other = jnp.where(d < half, d, jnp.where(d > half, d - 1, n_z - 1))
+    index = ((core_rel * n_z + jnp.where(core_rel == 1, d_other, d)) * 2 + xh_rel) * 6 + slots % 6
+    out = product(index.reshape(-1), rows.reshape(-1), a_pieces, mine, early, late)
     return out.reshape(MB * BLK, columns)
 
 

time: 105 us -> 127 us (1.21)
  local copies, waits for them, and re-layouts: 4.71 us -> 20.1 us
  other arithmetic: 1.08 us -> 6.81 us
  starting transfers between devices: 29.7 us -> 31.5 us
  Pallas kernels: 14.5 us -> 13.1 us
    unnamed x26 -> x15, local copies, waits for them, and re-layouts: 0.39 us -> 7 us
    ppermute x11 -> x5, waiting for transfers between devices: 1.44 us -> 6.24 us  [swap(): return lax.ppermute(block, axis, [(0, 1), (1, 0)])]
    ppermute x16, waiting for transfers between devices: 53 us -> 48.6 us  [shift(): lax.ppermute(block, axis, [(i, (i + distance) % n) for i in range(n)])]
    ppermute x16, starting transfers between devices: 24.5 us -> 27.3 us  [shift(): lax.ppermute(block, axis, [(i, (i + distance) % n) for i in range(n)])]
    another operation x3 -> x2, local copies, waits for them, and re-layouts: 0.13 us -> 2.08 us  [the longest x1 2 us: gather_b(): early = jnp.stack(by_offset[:half] + by_offset[half + 1:])]
    unnamed x3, other arithmetic: 0.06 us -> 1.8 us
    pallas_call x1, Pallas kernels: 14.5 us -> 13.1 us  [product(): pl.pallas_call(functools.partial(product_kernel, len(pieces)), out_shape=...]
    broadcast_in_dim x0 -> x4, local copies, waits for them, and re-layouts: none -> 1.3 us  [shards_body(): jnp.where(core_rel == 1, d_other, d)]
  transfers between devices with their start and end apart: 27 -> 21, of which waited for: 14 -> 9; matrix products, arithmetic and copies ran while one was open for 5% -> 21% of each run, Pallas kernels for 0% -> 0%
where the time goes in v2:
time: 127 us; the launch traced here: 126 us
  waiting for transfers between devices  54.8 us (43%)
  starting transfers between devices  31.5 us (25%)
  local copies, waits for them, and re-layouts  20.1 us (16%)
  Pallas kernels  13.1 us (10%)
  other arithmetic  6.81 us (5%)
    ppermute x16, waiting for transfers between devices, shift(): lax.ppermute(block, axis, [(i, (i + distance) % n) for i in range(n)])  48.6 us
    ppermute x16, starting transfers between devices, shift(): lax.ppermute(block, axis, [(i, (i + distance) % n) for i in range(n)])  27.3 us
    pallas_call x1, Pallas kernels, product(): pl.pallas_call(functools.partial(product_kernel, len(pieces)), out_shape=...  13.1 us
    unnamed x15, local copies, waits for them, and re-layouts  7 us
    ppermute x5, waiting for transfers between devices, swap(): return lax.ppermute(block, axis, [(0, 1), (1, 0)])  6.24 us
    ppermute x5, starting transfers between devices, swap(): return lax.ppermute(block, axis, [(0, 1), (1, 0)])  4.24 us
  transfers between devices with their start and end apart: 21, of which 9 were waited for; matrix products, arithmetic and copies ran while one was open for 21% of the time, Pallas kernels for 0%

profile of v2, /device:TPU:2, one launch (start us, length us, event | category | flops | bytes accessed | tf_op | source)
XLA Modules:
  0.0 126.5 jit_solution(18126730706416598719)
XLA Ops:
  0.0 2.1 %collective-permute-start.10 = (f32[6,64,128]{2,1,0:T(8,128)}, f32[6,64,128]{2,1,0:T(8,128)S(1)}, u32[]{:S(2)}, u32[]{:S(2)}) collective-permute-start(f32[6,64,128]{2,1,0:T(8,128)} %param.7), channel_id=1, source_target_pairs={{0,2},{2,0},{1,3},{3,1},{4,6},{6,4},{5,7},{7,5},{8,10},{10,8},{9,1... | collective-permute-start | bytes 589832 | tf_op jit(solution)/shard_map/ppermute | solution.py:21
  2.1 6.2 %collective-permute-done.10 = f32[6,64,128]{2,1,0:T(8,128)S(1)} collective-permute-done((f32[6,64,128]{2,1,0:T(8,128)}, f32[6,64,128]{2,1,0:T(8,128)S(1)}, u32[]{:S(2)}, u32[]{:S(2)}) %collective-permute-start.10) | collective-permute-done | bytes 196640 | tf_op jit(solution)/shard_map/ppermute | solution.py:21
  9.3 5.9 %collective-permute-start.11 = (f32[2,6,64,128]{3,2,1,0:T(8,128)S(1)}, f32[2,6,64,128]{3,2,1,0:T(8,128)}, u32[]{:S(2)}, u32[]{:S(2)}) collective-permute-start(f32[2,6,64,128]{3,2,1,0:T(8,128)S(1)} %pad_maximum_fusion.1), channel_id=1, source_target_pairs={{0,28},{4,0},{8,4},{12,8},{16,12},{20,16},{24,20},{28,24},{1,29},{... | collective-permute-start | bytes 1179656 | tf_op jit(solution)/shard_map/ppermute | solution.py:26
  15.2 7.5 %collective-permute-done.11 = f32[2,6,64,128]{3,2,1,0:T(8,128)} collective-permute-done((f32[2,6,64,128]{3,2,1,0:T(8,128)S(1)}, f32[2,6,64,128]{3,2,1,0:T(8,128)}, u32[]{:S(2)}, u32[]{:S(2)}) %collective-permute-start.11) | collective-permute-done | bytes 393248 | tf_op jit(solution)/shard_map/ppermute | solution.py:26
  22.8 3.8 %collective-permute-start.12 = (f32[2,6,64,128]{3,2,1,0:T(8,128)}, f32[2,6,64,128]{3,2,1,0:T(8,128)}, u32[]{:S(2)}, u32[]{:S(2)}) collective-permute-start(f32[2,6,64,128]{3,2,1,0:T(8,128)} %collective-permute-done.11), channel_id=1, source_target_pairs={{0,28},{4,0},{8,4},{12,8},{16,12},{20,16},{24,20},{28,24},{1,29},{... | collective-permute-start | bytes 1179656 | tf_op jit(solution)/shard_map/ppermute | solution.py:26
  31.2 1.6 %collective-permute-start.5 = (f32[16,64,128]{2,1,0:T(8,128)S(1)}, f32[16,64,128]{2,1,0:T(8,128)S(1)}, u32[]{:S(2)}, u32[]{:S(2)}) collective-permute-start(f32[16,64,128]{2,1,0:T(8,128)S(1)} %reshape.173), channel_id=1, source_target_pairs={{0,128},{128,0},{1,129},{129,1},{2,130},{130,2},{3,131},{131,3},{4... | collective-permute-start | bytes 1572872 | tf_op jit(solution)/shard_map/ppermute | solution.py:21
  35.3 3.2 %collective-permute-start.13 = (f32[2,6,64,128]{3,2,1,0:T(8,128)}, f32[2,6,64,128]{3,2,1,0:T(8,128)S(1)}, u32[]{:S(2)}, u32[]{:S(2)}) collective-permute-start(f32[2,6,64,128]{3,2,1,0:T(8,128)} %collective-permute-done.12), channel_id=1, source_target_pairs={{0,28},{4,0},{8,4},{12,8},{16,12},{20,16},{24,20},{28,24},{1,29},{... | collective-permute-start | bytes 1179656 | tf_op jit(solution)/shard_map/ppermute | solution.py:26
  38.5 2.0 %bitcast_dynamic-update-slice_fusion.11 = (f32[7,2,6,64,128]{4,3,2,1,0:T(8,128)}, f32[8,2,6,64,128]{4,3,2,1,0:T(8,128)}) fusion(f32[7,2,6,64,128]{4,3,2,1,0:T(8,128)} %get-tuple-element.25, f32[2,6,64,128]{3,2,1,0:T(8,128)} %collective-permute-done.11, f32[8,2,6,64,128]{4,3,2,1,0:T(8,128)} %get-tuple-element.26), kind=kLoop, calls=%fused_computation.17 | loop fusion | bytes 1179648
  40.4 2.2 %collective-permute-done.16 = f32[2,6,64,128]{3,2,1,0:T(8,128)S(1)} collective-permute-done((f32[2,6,64,128]{3,2,1,0:T(8,128)}, f32[2,6,64,128]{3,2,1,0:T(8,128)S(1)}, u32[]{:S(2)}, u32[]{:S(2)}) %collective-permute-start.16) | collective-permute-done | bytes 393248 | tf_op jit(solution)/shard_map/ppermute | solution.py:26
  42.7 2.0 %bitcast_dynamic-update-slice_fusion.9 = (f32[7,2,6,64,128]{4,3,2,1,0:T(8,128)}, f32[8,2,6,64,128]{4,3,2,1,0:T(8,128)}) fusion(f32[7,2,6,64,128]{4,3,2,1,0:T(8,128)} %get-tuple-element.23, f32[2,6,64,128]{3,2,1,0:T(8,128)} %collective-permute-done.12, f32[8,2,6,64,128]{4,3,2,1,0:T(8,128)} %get-tuple-element.24), kind=kLoop, calls=%fused_computation.15 | loop fusion | bytes 1179648
  44.7 3.3 %collective-permute-start.14 = (f32[6,64,128]{2,1,0:T(8,128)S(1)}, f32[6,64,128]{2,1,0:T(8,128)S(1)}, u32[]{:S(2)}, u32[]{:S(2)}) collective-permute-start(f32[6,64,128]{2,1,0:T(8,128)S(1)} %slice_bitcast_fusion.3), channel_id=1, source_target_pairs={{0,28},{4,0},{8,4},{12,8},{16,12},{20,16},{24,20},{28,24},{1,29},{... | collective-permute-start | bytes 589832 | tf_op jit(solution)/shard_map/ppermute | solution.py:26
  48.0 4.5 %collective-permute-done.17 = f32[2,6,64,128]{3,2,1,0:T(8,128)S(1)} collective-permute-done((f32[2,6,64,128]{3,2,1,0:T(8,128)S(1)}, f32[2,6,64,128]{3,2,1,0:T(8,128)S(1)}, u32[]{:S(2)}, u32[]{:S(2)}) %collective-permute-start.17) | collective-permute-done | bytes 393248 | tf_op jit(solution)/shard_map/ppermute | solution.py:26
  53.6 5.9 %collective-permute-done.18 = f32[6,64,128]{2,1,0:T(8,128)S(1)} collective-permute-done((f32[6,64,128]{2,1,0:T(8,128)S(1)}, f32[6,64,128]{2,1,0:T(8,128)S(1)}, u32[]{:S(2)}, u32[]{:S(2)}) %collective-permute-start.18) | collective-permute-done | bytes 196640 | tf_op jit(solution)/shard_map/ppermute | solution.py:26
  62.2 2.0 %bitcast_dynamic-update-slice_fusion = (f32[7,2,6,64,128]{4,3,2,1,0:T(8,128)}, f32[8,2,6,64,128]{4,3,2,1,0:T(8,128)}) fusion(f32[7,2,6,64,128]{4,3,2,1,0:T(8,128)} %get-tuple-element.15, f32[2,6,64,128]{3,2,1,0:T(8,128)} %collective-permute-done.15, f32[8,2,6,64,128]{4,3,2,1,0:T(8,128)} %get-tuple-element.16), kind=kLoop, calls=%fused_computation.6 | loop fusion | bytes 1179648 | tf_op jit(solution)/shard_map/stack | solution.py:63
  64.9 1.7 %collective-permute-start.1 = (s32[2,2,32]{2,1,0:T(2,128)S(1)}, s32[2,2,32]{2,1,0:T(2,128)S(1)}, u32[]{:S(2)}, u32[]{:S(2)}) collective-permute-start(s32[2,2,32]{2,1,0:T(2,128)S(1)} %pad_add_fusion), channel_id=1, source_target_pairs={{0,32},{32,64},{64,96},{96,0},{1,33},{33,65},{65,97},{97,1},{2,34}... | collective-permute-start | bytes 1544 | tf_op jit(solution)/shard_map/ppermute | solution.py:26
  66.6 1.7 %collective-permute-start.2 = (s32[2,2,32]{2,1,0:T(2,128)S(1)}, s32[2,2,32]{2,1,0:T(2,128)S(1)}, u32[]{:S(2)}, u32[]{:S(2)}) collective-permute-start(s32[2,2,32]{2,1,0:T(2,128)S(1)} %pad_add_fusion), channel_id=1, source_target_pairs={{0,96},{32,0},{64,32},{96,64},{1,97},{33,1},{65,33},{97,65},{2,98}... | collective-permute-start | bytes 1544 | tf_op jit(solution)/shard_map/ppermute | solution.py:26
  68.4 1.9 %collective-permute-start.7 = (f32[2,16,64,128]{3,2,1,0:T(8,128)S(1)}, f32[2,16,64,128]{3,2,1,0:T(8,128)S(1)}, u32[]{:S(2)}, u32[]{:S(2)}) collective-permute-start(f32[2,16,64,128]{3,2,1,0:T(8,128)S(1)} %pad_maximum_fusion), channel_id=1, source_target_pairs={{0,96},{32,0},{64,32},{96,64},{1,97},{33,1},{65,33},{97,65},{2,98}... | collective-permute-start | bytes 3145736 | tf_op jit(solution)/shard_map/ppermute | solution.py:26
  70.2 2.8 %collective-permute-start.3 = (s32[2,32]{1,0:T(2,128)S(1)}, s32[2,32]{1,0:T(2,128)S(1)}, u32[]{:S(2)}, u32[]{:S(2)}) collective-permute-start(s32[2,32]{1,0:T(2,128)S(1)} %slice_bitcast_fusion.5), channel_id=1, source_target_pairs={{0,96},{32,0},{64,32},{96,64},{1,97},{33,1},{65,33},{97,65},{2,98}... | collective-permute-start | bytes 776 | tf_op jit(solution)/shard_map/ppermute | solution.py:26
  73.8 19.8 %collective-permute-done.3 = s32[2,32]{1,0:T(2,128)S(1)} collective-permute-done((s32[2,32]{1,0:T(2,128)S(1)}, s32[2,32]{1,0:T(2,128)S(1)}, u32[]{:S(2)}, u32[]{:S(2)}) %collective-permute-start.3) | collective-permute-done | bytes 288 | tf_op jit(solution)/shard_map/ppermute | solution.py:26
  93.7 4.7 %collective-permute-done.4 = s32[2,32]{1,0:T(2,128)S(1)} collective-permute-done((s32[2,32]{1,0:T(2,128)S(1)}, s32[2,32]{1,0:T(2,128)S(1)}, u32[]{:S(2)}, u32[]{:S(2)}) %collective-permute-start.4) | collective-permute-done | bytes 288 | tf_op jit(solution)/shard_map/ppermute | solution.py:26
  100.0 2.0 %collective-permute-start.9 = (f32[16,64,128]{2,1,0:T(8,128)}, f32[16,64,128]{2,1,0:T(8,128)}, u32[]{:S(2)}, u32[]{:S(2)}) collective-permute-start(f32[16,64,128]{2,1,0:T(8,128)} %slice_bitcast_fusion), channel_id=1, source_target_pairs={{0,32},{32,64},{64,96},{96,0},{1,33},{33,65},{65,97},{97,1},{2,34}... | collective-permute-start | bytes 1572872 | tf_op jit(solution)/shard_map/ppermute | solution.py:26
  109.4 1.9 %collective-permute-done.8 = f32[16,64,128]{2,1,0:T(8,128)} collective-permute-done((f32[16,64,128]{2,1,0:T(8,128)}, f32[16,64,128]{2,1,0:T(8,128)}, u32[]{:S(2)}, u32[]{:S(2)}) %collective-permute-start.8) | collective-permute-done | bytes 524320 | tf_op jit(solution)/shard_map/ppermute | solution.py:26
  111.4 2.0 %collective-permute-done.9 = f32[16,64,128]{2,1,0:T(8,128)} collective-permute-done((f32[16,64,128]{2,1,0:T(8,128)}, f32[16,64,128]{2,1,0:T(8,128)}, u32[]{:S(2)}, u32[]{:S(2)}) %collective-permute-start.9) | collective-permute-done | bytes 524320 | tf_op jit(solution)/shard_map/ppermute | solution.py:26
  113.4 13.1 %shard_map.46 = f32[32,64,128]{2,1,0:T(8,128)} custom-call(s32[256]{0:T(256)S(1)} %fusion.5.index_ref, s32[256]{0:T(256)S(1)} %reshape_squeeze.6.rows_ref, f32[1,16,64,128]{3,2,1,0:T(8,128)S(1)} %broadcast_in_dim_reshape.3.refs_0_, f32[1,16,64,128]{3,2,1,0:T(8,128)S(1)} %bitcast.71, f32[2,16,64,128]{3,2,1,0:T(8,128)S(1)} %collective-permute-done.6.refs_2_, ...), custom_call_target="tpu_custom_call" | custom-call | flops 268435456 | bytes 11534336 | tf_op jit(solution)/shard_map/pallas_call | solution.py:124
  (69 shorter events, 22.5 us)
Async XLA Ops:
  0.0 8.4 %collective-permute-start.10 = (f32[6,64,128]{2,1,0:T(8,128)}, f32[6,64,128]{2,1,0:T(8,128)S(1)}, u32[]{:S(2)}, u32[]{:S(2)}) collective-permute-start(f32[6,64,128]{2,1,0:T(8,128)} %param.7), channel_id=1, source_target_pairs={{0,2},{2,0},{1,3},{3,1},{4,6},{6,4},{5,7},{7,5},{8,10},{10,8},{9,1... | collective-permute-start | bytes 589832 | tf_op jit(solution)/shard_map/ppermute | solution.py:21
  9.3 13.5 %collective-permute-start.11 = (f32[2,6,64,128]{3,2,1,0:T(8,128)S(1)}, f32[2,6,64,128]{3,2,1,0:T(8,128)}, u32[]{:S(2)}, u32[]{:S(2)}) collective-permute-start(f32[2,6,64,128]{3,2,1,0:T(8,128)S(1)} %pad_maximum_fusion.1), channel_id=1, source_target_pairs={{0,28},{4,0},{8,4},{12,8},{16,12},{20,16},{24,20},{28,24},{1,29},{... | collective-permute-start | bytes 1179656 | tf_op jit(solution)/shard_map/ppermute | solution.py:26
  15.2 17.6 %collective-permute-start.15 = (f32[2,6,64,128]{3,2,1,0:T(8,128)S(1)}, f32[2,6,64,128]{3,2,1,0:T(8,128)}, u32[]{:S(2)}, u32[]{:S(2)}) collective-permute-start(f32[2,6,64,128]{3,2,1,0:T(8,128)S(1)} %pad_maximum_fusion.1), channel_id=1, source_target_pairs={{0,4},{4,8},{8,12},{12,16},{16,20},{20,24},{24,28},{28,0},{1,5},{5... | collective-permute-start | bytes 1179656 | tf_op jit(solution)/shard_map/ppermute | solution.py:26
  22.8 12.5 %collective-permute-start.12 = (f32[2,6,64,128]{3,2,1,0:T(8,128)}, f32[2,6,64,128]{3,2,1,0:T(8,128)}, u32[]{:S(2)}, u32[]{:S(2)}) collective-permute-start(f32[2,6,64,128]{3,2,1,0:T(8,128)} %collective-permute-done.11), channel_id=1, source_target_pairs={{0,28},{4,0},{8,4},{12,8},{16,12},{20,16},{24,20},{28,24},{1,29},{... | collective-permute-start | bytes 1179656 | tf_op jit(solution)/shard_map/ppermute | solution.py:26
  27.8 6.4 %copy-start = (f32[6,64,128]{2,1,0:T(8,128)S(1)}, f32[6,64,128]{2,1,0:T(8,128)}, u32[]{:S(2)}) copy-start(f32[6,64,128]{2,1,0:T(8,128)} %param.7) | copy-start | bytes 589828
  27.8 37.1 %collective-permute-start = (s32[2,32]{1,0:T(2,128)}, s32[2,32]{1,0:T(2,128)S(1)}, u32[]{:S(2)}, u32[]{:S(2)}) collective-permute-start(s32[2,32]{1,0:T(2,128)} %get-tuple-element.28), channel_id=1, source_target_pairs={{0,128},{128,0},{1,129},{129,1},{2,130},{130,2},{3,131},{131,3},{4... | collective-permute-start | bytes 776 | tf_op jit(solution)/shard_map/ppermute | solution.py:21
  31.2 37.1 %collective-permute-start.5 = (f32[16,64,128]{2,1,0:T(8,128)S(1)}, f32[16,64,128]{2,1,0:T(8,128)S(1)}, u32[]{:S(2)}, u32[]{:S(2)}) collective-permute-start(f32[16,64,128]{2,1,0:T(8,128)S(1)} %reshape.173), channel_id=1, source_target_pairs={{0,128},{128,0},{1,129},{129,1},{2,130},{130,2},{3,131},{131,3},{4... | collective-permute-start | bytes 1572872 | tf_op jit(solution)/shard_map/ppermute | solution.py:21
  32.9 9.8 %collective-permute-start.16 = (f32[2,6,64,128]{3,2,1,0:T(8,128)}, f32[2,6,64,128]{3,2,1,0:T(8,128)S(1)}, u32[]{:S(2)}, u32[]{:S(2)}) collective-permute-start(f32[2,6,64,128]{3,2,1,0:T(8,128)} %collective-permute-done.15), channel_id=1, source_target_pairs={{0,4},{4,8},{8,12},{12,16},{16,20},{20,24},{24,28},{28,0},{1,5},{5... | collective-permute-start | bytes 1179656 | tf_op jit(solution)/shard_map/ppermute | solution.py:26
  35.3 9.4 %collective-permute-start.13 = (f32[2,6,64,128]{3,2,1,0:T(8,128)}, f32[2,6,64,128]{3,2,1,0:T(8,128)S(1)}, u32[]{:S(2)}, u32[]{:S(2)}) collective-permute-start(f32[2,6,64,128]{3,2,1,0:T(8,128)} %collective-permute-done.12), channel_id=1, source_target_pairs={{0,28},{4,0},{8,4},{12,8},{16,12},{20,16},{24,20},{28,24},{1,29},{... | collective-permute-start | bytes 1179656 | tf_op jit(solution)/shard_map/ppermute | solution.py:26
  42.7 9.8 %collective-permute-start.17 = (f32[2,6,64,128]{3,2,1,0:T(8,128)S(1)}, f32[2,6,64,128]{3,2,1,0:T(8,128)S(1)}, u32[]{:S(2)}, u32[]{:S(2)}) collective-permute-start(f32[2,6,64,128]{3,2,1,0:T(8,128)S(1)} %collective-permute-done.16), channel_id=1, source_target_pairs={{0,4},{4,8},{8,12},{12,16},{16,20},{20,24},{24,28},{28,0},{1,5},{5... | collective-permute-start | bytes 1179656 | tf_op jit(solution)/shard_map/ppermute | solution.py:26
  44.7 19.6 %copy-start.1 = (s32[1,1,32]{2,1,0:T(1,128)S(1)}, s32[1,1,32]{2,1,0:T(1,128)}, u32[]{:S(2)}) copy-start(s32[1,1,32]{2,1,0:T(1,128)} %param.6) | copy-start | bytes 388
  44.7 19.6 %copy-start.2 = (s32[1,1,32]{2,1,0:T(1,128)S(1)}, s32[1,1,32]{2,1,0:T(1,128)}, u32[]{:S(2)}) copy-start(s32[1,1,32]{2,1,0:T(1,128)} %param.5) | copy-start | bytes 388
  44.7 8.9 %collective-permute-start.14 = (f32[6,64,128]{2,1,0:T(8,128)S(1)}, f32[6,64,128]{2,1,0:T(8,128)S(1)}, u32[]{:S(2)}, u32[]{:S(2)}) collective-permute-start(f32[6,64,128]{2,1,0:T(8,128)S(1)} %slice_bitcast_fusion.3), channel_id=1, source_target_pairs={{0,28},{4,0},{8,4},{12,8},{16,12},{20,16},{24,20},{28,24},{1,29},{... | collective-permute-start | bytes 589832 | tf_op jit(solution)/shard_map/ppermute | solution.py:26
  52.5 7.0 %collective-permute-start.18 = (f32[6,64,128]{2,1,0:T(8,128)S(1)}, f32[6,64,128]{2,1,0:T(8,128)S(1)}, u32[]{:S(2)}, u32[]{:S(2)}) collective-permute-start(f32[6,64,128]{2,1,0:T(8,128)S(1)} %slice_bitcast_fusion.2), channel_id=1, source_target_pairs={{0,4},{4,8},{8,12},{12,16},{16,20},{20,24},{24,28},{28,0},{1,5},{5... | collective-permute-start | bytes 589832 | tf_op jit(solution)/shard_map/ppermute | solution.py:26
  64.2 49.2 %collective-permute-start.19 = (f32[7,2,6,64,128]{4,3,2,1,0:T(8,128)}, f32[7,2,6,64,128]{4,3,2,1,0:T(8,128)}, u32[]{:S(2)}, u32[]{:S(2)}) collective-permute-start(f32[7,2,6,64,128]{4,3,2,1,0:T(8,128)} %get-tuple-element.13), channel_id=1, source_target_pairs={{0,1},{1,0},{2,3},{3,2},{4,5},{5,4},{6,7},{7,6},{8,9},{9,8},{10,11... | collective-permute-start | bytes 8257544 | tf_op jit(solution)/shard_map/ppermute | solution.py:21
  64.9 8.2 %collective-permute-start.1 = (s32[2,2,32]{2,1,0:T(2,128)S(1)}, s32[2,2,32]{2,1,0:T(2,128)S(1)}, u32[]{:S(2)}, u32[]{:S(2)}) collective-permute-start(s32[2,2,32]{2,1,0:T(2,128)S(1)} %pad_add_fusion), channel_id=1, source_target_pairs={{0,32},{32,64},{64,96},{96,0},{1,33},{33,65},{65,97},{97,1},{2,34}... | collective-permute-start | bytes 1544 | tf_op jit(solution)/shard_map/ppermute | solution.py:26
  66.6 3.6 %collective-permute-start.2 = (s32[2,2,32]{2,1,0:T(2,128)S(1)}, s32[2,2,32]{2,1,0:T(2,128)S(1)}, u32[]{:S(2)}, u32[]{:S(2)}) collective-permute-start(s32[2,2,32]{2,1,0:T(2,128)S(1)} %pad_add_fusion), channel_id=1, source_target_pairs={{0,96},{32,0},{64,32},{96,64},{1,97},{33,1},{65,33},{97,65},{2,98}... | collective-permute-start | bytes 1544 | tf_op jit(solution)/shard_map/ppermute | solution.py:26
  68.4 30.0 %collective-permute-start.7 = (f32[2,16,64,128]{3,2,1,0:T(8,128)S(1)}, f32[2,16,64,128]{3,2,1,0:T(8,128)S(1)}, u32[]{:S(2)}, u32[]{:S(2)}) collective-permute-start(f32[2,16,64,128]{3,2,1,0:T(8,128)S(1)} %pad_maximum_fusion), channel_id=1, source_target_pairs={{0,96},{32,0},{64,32},{96,64},{1,97},{33,1},{65,33},{97,65},{2,98}... | collective-permute-start | bytes 3145736 | tf_op jit(solution)/shard_map/ppermute | solution.py:26
  70.2 23.4 %collective-permute-start.3 = (s32[2,32]{1,0:T(2,128)S(1)}, s32[2,32]{1,0:T(2,128)S(1)}, u32[]{:S(2)}, u32[]{:S(2)}) collective-permute-start(s32[2,32]{1,0:T(2,128)S(1)} %slice_bitcast_fusion.5), channel_id=1, source_target_pairs={{0,96},{32,0},{64,32},{96,64},{1,97},{33,1},{65,33},{97,65},{2,98}... | collective-permute-start | bytes 776 | tf_op jit(solution)/shard_map/ppermute | solution.py:26
  73.1 26.1 %collective-permute-start.6 = (f32[2,16,64,128]{3,2,1,0:T(8,128)S(1)}, f32[2,16,64,128]{3,2,1,0:T(8,128)S(1)}, u32[]{:S(2)}, u32[]{:S(2)}) collective-permute-start(f32[2,16,64,128]{3,2,1,0:T(8,128)S(1)} %pad_maximum_fusion), channel_id=1, source_target_pairs={{0,32},{32,64},{64,96},{96,0},{1,33},{33,65},{65,97},{97,1},{2,34}... | collective-permute-start | bytes 3145736 | tf_op jit(solution)/shard_map/ppermute | solution.py:26
  73.1 25.3 %collective-permute-start.4 = (s32[2,32]{1,0:T(2,128)S(1)}, s32[2,32]{1,0:T(2,128)S(1)}, u32[]{:S(2)}, u32[]{:S(2)}) collective-permute-start(s32[2,32]{1,0:T(2,128)S(1)} %slice_bitcast_fusion.4), channel_id=1, source_target_pairs={{0,32},{32,64},{64,96},{96,0},{1,33},{33,65},{65,97},{97,1},{2,34}... | collective-permute-start | bytes 776 | tf_op jit(solution)/shard_map/ppermute | solution.py:26
  99.2 12.2 %collective-permute-start.8 = (f32[16,64,128]{2,1,0:T(8,128)}, f32[16,64,128]{2,1,0:T(8,128)}, u32[]{:S(2)}, u32[]{:S(2)}) collective-permute-start(f32[16,64,128]{2,1,0:T(8,128)} %slice_bitcast_fusion.1), channel_id=1, source_target_pairs={{0,96},{32,0},{64,32},{96,64},{1,97},{33,1},{65,33},{97,65},{2,98}... | collective-permute-start | bytes 1572872 | tf_op jit(solution)/shard_map/ppermute | solution.py:26
  100.0 13.4 %collective-permute-start.9 = (f32[16,64,128]{2,1,0:T(8,128)}, f32[16,64,128]{2,1,0:T(8,128)}, u32[]{:S(2)}, u32[]{:S(2)}) collective-permute-start(f32[16,64,128]{2,1,0:T(8,128)} %slice_bitcast_fusion), channel_id=1, source_target_pairs={{0,32},{32,64},{64,96},{96,0},{1,33},{33,65},{65,97},{97,1},{2,34}... | collective-permute-start | bytes 1572872 | tf_op jit(solution)/shard_map/ppermute | solution.py:26
  102.8 6.6 %collective-permute-start.20 = (f32[2,6,64,128]{3,2,1,0:T(8,128)}, f32[2,6,64,128]{3,2,1,0:T(8,128)S(1)}, u32[]{:S(2)}, u32[]{:S(2)}) collective-permute-start(f32[2,6,64,128]{3,2,1,0:T(8,128)} %pad_maximum_fusion.2), channel_id=1, source_target_pairs={{0,1},{1,0},{2,3},{3,2},{4,5},{5,4},{6,7},{7,6},{8,9},{9,8},{10,11... | collective-permute-start | bytes 1179656 | tf_op jit(solution)/shard_map/ppermute | solution.py:21

commit v3 on v0

--- a/solution.py
+++ b/solution.py
@@ -60,8 +60,7 @@
     far_down = shift(down[1], "z", 1)
     by_offset[half] = jnp.stack([far_up, far_down])
     mine = jnp.stack(by_offset)
-    other = jnp.stack([swap(piece, "core") for piece in by_offset])
-    return mine, other
+    return mine, swap(mine, "core")
 
 
 def product_kernel(n_pieces, index_ref, rows_ref, *refs):
@@ -81,6 +80,8 @@
                 pair = a_ref[j, t]
                 pair_hi = pair.astype(jnp.bfloat16)
                 pair_lo = (pair - pair_hi.astype(jnp.float32)).astype(jnp.bfloat16)
+                both = jnp.concatenate([pair_hi, pair_lo], axis=0)
+                rows_a = pair.shape[0]
                 for u in range(2):
                     g = base + 2 * t + u
                     row = jnp.minimum(rows_ref[g], blocks)
@@ -94,13 +95,14 @@
                     pieces_lo = [right_lo, zeros] if u == 0 else [zeros, right_lo]
                     right_hi = jnp.concatenate(pieces_hi, axis=0)
                     right_lo = jnp.concatenate(pieces_lo, axis=0)
-                    term = jnp.dot(pair_hi, right_hi, preferred_element_type=jnp.float32)
+                    with_hi = jnp.dot(both, right_hi, preferred_element_type=jnp.float32)
+                    term = with_hi[:rows_a]
                     term += jnp.dot(pair_hi, right_lo, preferred_element_type=jnp.float32)
-                    term += jnp.dot(pair_lo, right_hi, preferred_element_type=jnp.float32)
+                    term += with_hi[rows_a:]
                     acc_ref[row] += term
                 return carry
 
-            lax.fori_loop(0, n_pairs, one_pair, 0, unroll=4)
+            lax.fori_loop(0, n_pairs, one_pair, 0, unroll=16)
             panel += 1
     out_ref[...] = acc_ref[:blocks]
 

time: 105 us -> 127 us (1.21)
  waiting for transfers between devices: 54.5 us -> 72.9 us
  Pallas kernels: 14.5 us -> 8.38 us
  local copies, waits for them, and re-layouts: 4.71 us -> 9.52 us
  starting transfers between devices: 29.7 us -> 32.6 us
  other arithmetic: 1.08 us -> 3.69 us
    ppermute x11 -> x4, waiting for transfers between devices: 1.44 us -> 17.6 us  [swap(): return lax.ppermute(block, axis, [(0, 1), (1, 0)])]
    pallas_call x1, Pallas kernels: 14.5 us -> 8.38 us  [product(): pl.pallas_call(functools.partial(product_kernel, len(pieces)), out_shape=...]
    ppermute x16, starting transfers between devices: 24.5 us -> 28.3 us  [shift(): lax.ppermute(block, axis, [(i, (i + distance) % n) for i in range(n)])]
    unnamed x26 -> x15, local copies, waits for them, and re-layouts: 0.39 us -> 3.96 us
    unnamed x3, other arithmetic: 0.06 us -> 2.51 us
    ppermute x16, waiting for transfers between devices: 53 us -> 55.2 us  [shift(): lax.ppermute(block, axis, [(i, (i + distance) % n) for i in range(n)])]
    ppermute x11 -> x4, starting transfers between devices: 5.13 us -> 4.33 us  [swap(): return lax.ppermute(block, axis, [(0, 1), (1, 0)])]
  transfers between devices with their start and end apart: 27 -> 20, of which waited for: 14 -> 11; matrix products, arithmetic and copies ran while one was open for 5% -> 7% of each run, Pallas kernels for 0% -> 0%
where the time goes in v3:
time: 127 us
  waiting for transfers between devices  72.9 us (57%)
  starting transfers between devices  32.6 us (26%)
  local copies, waits for them, and re-layouts  9.52 us (7%)
  Pallas kernels  8.38 us (7%)
  other arithmetic  3.69 us (3%)
    ppermute x16, waiting for transfers between devices, shift(): lax.ppermute(block, axis, [(i, (i + distance) % n) for i in range(n)])  55.2 us
    ppermute x16, starting transfers between devices, shift(): lax.ppermute(block, axis, [(i, (i + distance) % n) for i in range(n)])  28.3 us
    ppermute x4, waiting for transfers between devices, swap(): return lax.ppermute(block, axis, [(0, 1), (1, 0)])  17.6 us
    pallas_call x1, Pallas kernels, product(): pl.pallas_call(functools.partial(product_kernel, len(pieces)), out_shape=...  8.38 us
    ppermute x4, starting transfers between devices, swap(): return lax.ppermute(block, axis, [(0, 1), (1, 0)])  4.33 us
    unnamed x15, local copies, waits for them, and re-layouts  3.96 us
  transfers between devices with their start and end apart: 20, of which 11 were waited for; matrix products, arithmetic and copies ran while one was open for 7% of the time, Pallas kernels for 0%

profile of v3, /device:TPU:2, one launch (start us, length us, event | category | flops | bytes accessed | tf_op | source)
XLA Modules:
  0.0 127.2 jit_solution(1939097186188885512)
XLA Ops:
  0.0 2.1 %collective-permute-start.10 = (f32[6,64,128]{2,1,0:T(8,128)}, f32[6,64,128]{2,1,0:T(8,128)S(1)}, u32[]{:S(2)}, u32[]{:S(2)}) collective-permute-start(f32[6,64,128]{2,1,0:T(8,128)} %param.7), channel_id=1, source_target_pairs={{0,2},{2,0},{1,3},{3,1},{4,6},{6,4},{5,7},{7,5},{8,10},{10,8},{9,1... | collective-permute-start | bytes 589832 | tf_op jit(solution)/shard_map/ppermute | solution.py:21
  2.1 6.2 %collective-permute-done.10 = f32[6,64,128]{2,1,0:T(8,128)S(1)} collective-permute-done((f32[6,64,128]{2,1,0:T(8,128)}, f32[6,64,128]{2,1,0:T(8,128)S(1)}, u32[]{:S(2)}, u32[]{:S(2)}) %collective-permute-start.10) | collective-permute-done | bytes 196640 | tf_op jit(solution)/shard_map/ppermute | solution.py:21
  8.4 1.0 pad_maximum_fusion.1
  9.3 5.9 %collective-permute-start.11 = (f32[2,6,64,128]{3,2,1,0:T(8,128)S(1)}, f32[2,6,64,128]{3,2,1,0:T(8,128)S(1)}, u32[]{:S(2)}, u32[]{:S(2)}) collective-permute-start(f32[2,6,64,128]{3,2,1,0:T(8,128)S(1)} %pad_maximum_fusion.1), channel_id=1, source_target_pairs={{0,28},{4,0},{8,4},{12,8},{16,12},{20,16},{24,20},{28,24},{1,29},{... | collective-permute-start | bytes 1179656 | tf_op jit(solution)/shard_map/ppermute | solution.py:26
  15.2 7.5 %collective-permute-done.11 = f32[2,6,64,128]{3,2,1,0:T(8,128)S(1)} collective-permute-done((f32[2,6,64,128]{3,2,1,0:T(8,128)S(1)}, f32[2,6,64,128]{3,2,1,0:T(8,128)S(1)}, u32[]{:S(2)}, u32[]{:S(2)}) %collective-permute-start.11) | collective-permute-done | bytes 393248 | tf_op jit(solution)/shard_map/ppermute | solution.py:26
  22.8 3.7 %collective-permute-start.12 = (f32[2,6,64,128]{3,2,1,0:T(8,128)S(1)}, f32[2,6,64,128]{3,2,1,0:T(8,128)S(1)}, u32[]{:S(2)}, u32[]{:S(2)}) collective-permute-start(f32[2,6,64,128]{3,2,1,0:T(8,128)S(1)} %collective-permute-done.11), channel_id=1, source_target_pairs={{0,28},{4,0},{8,4},{12,8},{16,12},{20,16},{24,20},{28,24},{1,29},{... | collective-permute-start | bytes 1179656 | tf_op jit(solution)/shard_map/ppermute | solution.py:26
  26.5 1.7 %bitcast_dynamic-update-slice_fusion.6 = f32[8,2,6,64,128]{4,3,2,1,0:T(8,128)} fusion(f32[1,6,64,128]{3,2,1,0:T(8,128)S(1)} %bitcast.71, f32[1,6,64,128]{3,2,1,0:T(8,128)} %bitcast.69), kind=kLoop, calls=%fused_computation.13 | loop fusion | flops 98303 | bytes 786432
  28.2 5.0 %collective-permute-done.12 = f32[2,6,64,128]{3,2,1,0:T(8,128)S(1)} collective-permute-done((f32[2,6,64,128]{3,2,1,0:T(8,128)S(1)}, f32[2,6,64,128]{3,2,1,0:T(8,128)S(1)}, u32[]{:S(2)}, u32[]{:S(2)}) %collective-permute-start.12) | collective-permute-done | bytes 393248 | tf_op jit(solution)/shard_map/ppermute | solution.py:26
  33.1 3.7 %collective-permute-start.13 = (f32[2,6,64,128]{3,2,1,0:T(8,128)S(1)}, f32[2,6,64,128]{3,2,1,0:T(8,128)S(1)}, u32[]{:S(2)}, u32[]{:S(2)}) collective-permute-start(f32[2,6,64,128]{3,2,1,0:T(8,128)S(1)} %collective-permute-done.12), channel_id=1, source_target_pairs={{0,28},{4,0},{8,4},{12,8},{16,12},{20,16},{24,20},{28,24},{1,29},{... | collective-permute-start | bytes 1179656 | tf_op jit(solution)/shard_map/ppermute | solution.py:26
  38.4 4.3 %collective-permute-done.13 = f32[2,6,64,128]{3,2,1,0:T(8,128)S(1)} collective-permute-done((f32[2,6,64,128]{3,2,1,0:T(8,128)S(1)}, f32[2,6,64,128]{3,2,1,0:T(8,128)S(1)}, u32[]{:S(2)}, u32[]{:S(2)}) %collective-permute-start.13) | collective-permute-done | bytes 393248 | tf_op jit(solution)/shard_map/ppermute | solution.py:26
  42.6 3.8 %collective-permute-start.14 = (f32[6,64,128]{2,1,0:T(8,128)S(1)}, f32[6,64,128]{2,1,0:T(8,128)S(1)}, u32[]{:S(2)}, u32[]{:S(2)}) collective-permute-start(f32[6,64,128]{2,1,0:T(8,128)S(1)} %slice_bitcast_fusion.3), channel_id=1, source_target_pairs={{0,28},{4,0},{8,4},{12,8},{16,12},{20,16},{24,20},{28,24},{1,29},{... | collective-permute-start | bytes 589832 | tf_op jit(solution)/shard_map/ppermute | solution.py:26
  47.7 1.9 %collective-permute-done.14 = f32[6,64,128]{2,1,0:T(8,128)S(1)} collective-permute-done((f32[6,64,128]{2,1,0:T(8,128)S(1)}, f32[6,64,128]{2,1,0:T(8,128)S(1)}, u32[]{:S(2)}, u32[]{:S(2)}) %collective-permute-start.14) | collective-permute-done | bytes 196640 | tf_op jit(solution)/shard_map/ppermute | solution.py:26
  49.6 4.2 %collective-permute-done.18 = f32[6,64,128]{2,1,0:T(8,128)S(1)} collective-permute-done((f32[6,64,128]{2,1,0:T(8,128)S(1)}, f32[6,64,128]{2,1,0:T(8,128)S(1)}, u32[]{:S(2)}, u32[]{:S(2)}) %collective-permute-start.18) | collective-permute-done | bytes 196640 | tf_op jit(solution)/shard_map/ppermute | solution.py:26
  59.4 1.6 %collective-permute-start = (s32[2,32]{1,0:T(2,128)S(1)}, s32[2,32]{1,0:T(2,128)S(1)}, u32[]{:S(2)}, u32[]{:S(2)}) collective-permute-start(s32[2,32]{1,0:T(2,128)S(1)} %get-tuple-element.12), channel_id=1, source_target_pairs={{0,128},{128,0},{1,129},{129,1},{2,130},{130,2},{3,131},{131,3},{4... | collective-permute-start | bytes 776 | tf_op jit(solution)/shard_map/ppermute | solution.py:21
  61.8 11.4 %collective-permute-done = s32[2,32]{1,0:T(2,128)S(1)} collective-permute-done((s32[2,32]{1,0:T(2,128)S(1)}, s32[2,32]{1,0:T(2,128)S(1)}, u32[]{:S(2)}, u32[]{:S(2)}) %collective-permute-start) | collective-permute-done | bytes 288 | tf_op jit(solution)/shard_map/ppermute | solution.py:21
  73.3 1.6 %collective-permute-start.1 = (s32[2,2,32]{2,1,0:T(2,128)S(1)}, s32[2,2,32]{2,1,0:T(2,128)S(1)}, u32[]{:S(2)}, u32[]{:S(2)}) collective-permute-start(s32[2,2,32]{2,1,0:T(2,128)S(1)} %pad_add_fusion), channel_id=1, source_target_pairs={{0,32},{32,64},{64,96},{96,0},{1,33},{33,65},{65,97},{97,1},{2,34}... | collective-permute-start | bytes 1544 | tf_op jit(solution)/shard_map/ppermute | solution.py:26
  74.8 1.7 %collective-permute-start.2 = (s32[2,2,32]{2,1,0:T(2,128)S(1)}, s32[2,2,32]{2,1,0:T(2,128)S(1)}, u32[]{:S(2)}, u32[]{:S(2)}) collective-permute-start(s32[2,2,32]{2,1,0:T(2,128)S(1)} %pad_add_fusion), channel_id=1, source_target_pairs={{0,96},{32,0},{64,32},{96,64},{1,97},{33,1},{65,33},{97,65},{2,98}... | collective-permute-start | bytes 1544 | tf_op jit(solution)/shard_map/ppermute | solution.py:26
  76.6 1.8 %collective-permute-start.7 = (f32[2,16,64,128]{3,2,1,0:T(8,128)S(1)}, f32[2,16,64,128]{3,2,1,0:T(8,128)S(1)}, u32[]{:S(2)}, u32[]{:S(2)}) collective-permute-start(f32[2,16,64,128]{3,2,1,0:T(8,128)S(1)} %pad_maximum_fusion), channel_id=1, source_target_pairs={{0,96},{32,0},{64,32},{96,64},{1,97},{33,1},{65,33},{97,65},{2,98}... | collective-permute-start | bytes 3145736 | tf_op jit(solution)/shard_map/ppermute | solution.py:26
  78.7 3.0 %collective-permute-start.3 = (s32[2,32]{1,0:T(2,128)S(1)}, s32[2,32]{1,0:T(2,128)S(1)}, u32[]{:S(2)}, u32[]{:S(2)}) collective-permute-start(s32[2,32]{1,0:T(2,128)S(1)} %slice_bitcast_fusion.5), channel_id=1, source_target_pairs={{0,96},{32,0},{64,32},{96,64},{1,97},{33,1},{65,33},{97,65},{2,98}... | collective-permute-start | bytes 776 | tf_op jit(solution)/shard_map/ppermute | solution.py:26
  81.7 19.4 %collective-permute-done.3 = s32[2,32]{1,0:T(2,128)S(1)} collective-permute-done((s32[2,32]{1,0:T(2,128)S(1)}, s32[2,32]{1,0:T(2,128)S(1)}, u32[]{:S(2)}, u32[]{:S(2)}) %collective-permute-start.3) | collective-permute-done | bytes 288 | tf_op jit(solution)/shard_map/ppermute | solution.py:26
  102.0 2.7 %collective-permute-start.8 = (f32[16,64,128]{2,1,0:T(8,128)}, f32[16,64,128]{2,1,0:T(8,128)}, u32[]{:S(2)}, u32[]{:S(2)}) collective-permute-start(f32[16,64,128]{2,1,0:T(8,128)} %slice_bitcast_fusion.1), channel_id=1, source_target_pairs={{0,96},{32,0},{64,32},{96,64},{1,97},{33,1},{65,33},{97,65},{2,98}... | collective-permute-start | bytes 1572872 | tf_op jit(solution)/shard_map/ppermute | solution.py:26
  106.2 8.4 %collective-permute-done.8 = f32[16,64,128]{2,1,0:T(8,128)} collective-permute-done((f32[16,64,128]{2,1,0:T(8,128)}, f32[16,64,128]{2,1,0:T(8,128)}, u32[]{:S(2)}, u32[]{:S(2)}) %collective-permute-start.8) | collective-permute-done | bytes 524320 | tf_op jit(solution)/shard_map/ppermute | solution.py:26
  114.6 4.2 %collective-permute-done.9 = f32[16,64,128]{2,1,0:T(8,128)} collective-permute-done((f32[16,64,128]{2,1,0:T(8,128)}, f32[16,64,128]{2,1,0:T(8,128)}, u32[]{:S(2)}, u32[]{:S(2)}) %collective-permute-start.9) | collective-permute-done | bytes 524320 | tf_op jit(solution)/shard_map/ppermute | solution.py:26
  118.8 8.4 %shard_map.46 = f32[32,64,128]{2,1,0:T(8,128)} custom-call(s32[256]{0:T(256)S(1)} %fusion.6.index_ref, s32[256]{0:T(256)S(1)} %reshape_squeeze.6.rows_ref, f32[1,16,64,128]{3,2,1,0:T(8,128)S(1)} %broadcast_in_dim_reshape.3.refs_0_, f32[1,16,64,128]{3,2,1,0:T(8,128)S(1)} %bitcast.65, f32[2,16,64,128]{3,2,1,0:T(8,128)S(1)} %collective-permute-done.6.refs_2_, ...), custom_call_target="tpu_custom_call" | custom-call | flops 268435456 | bytes 11534336 | tf_op jit(solution)/shard_map/pallas_call | solution.py:116
  (64 shorter events, 12.0 us)
Async XLA Ops:
  0.0 8.4 %collective-permute-start.10 = (f32[6,64,128]{2,1,0:T(8,128)}, f32[6,64,128]{2,1,0:T(8,128)S(1)}, u32[]{:S(2)}, u32[]{:S(2)}) collective-permute-start(f32[6,64,128]{2,1,0:T(8,128)} %param.7), channel_id=1, source_target_pairs={{0,2},{2,0},{1,3},{3,1},{4,6},{6,4},{5,7},{7,5},{8,10},{10,8},{9,1... | collective-permute-start | bytes 589832 | tf_op jit(solution)/shard_map/ppermute | solution.py:21
  9.3 13.5 %collective-permute-start.11 = (f32[2,6,64,128]{3,2,1,0:T(8,128)S(1)}, f32[2,6,64,128]{3,2,1,0:T(8,128)S(1)}, u32[]{:S(2)}, u32[]{:S(2)}) collective-permute-start(f32[2,6,64,128]{3,2,1,0:T(8,128)S(1)} %pad_maximum_fusion.1), channel_id=1, source_target_pairs={{0,28},{4,0},{8,4},{12,8},{16,12},{20,16},{24,20},{28,24},{1,29},{... | collective-permute-start | bytes 1179656 | tf_op jit(solution)/shard_map/ppermute | solution.py:26
  15.2 11.2 %collective-permute-start.15 = (f32[2,6,64,128]{3,2,1,0:T(8,128)S(1)}, f32[2,6,64,128]{3,2,1,0:T(8,128)S(1)}, u32[]{:S(2)}, u32[]{:S(2)}) collective-permute-start(f32[2,6,64,128]{3,2,1,0:T(8,128)S(1)} %pad_maximum_fusion.1), channel_id=1, source_target_pairs={{0,4},{4,8},{8,12},{12,16},{16,20},{20,24},{24,28},{28,0},{1,5},{5... | collective-permute-start | bytes 1179656 | tf_op jit(solution)/shard_map/ppermute | solution.py:26
  22.8 10.4 %collective-permute-start.12 = (f32[2,6,64,128]{3,2,1,0:T(8,128)S(1)}, f32[2,6,64,128]{3,2,1,0:T(8,128)S(1)}, u32[]{:S(2)}, u32[]{:S(2)}) collective-permute-start(f32[2,6,64,128]{3,2,1,0:T(8,128)S(1)} %collective-permute-done.11), channel_id=1, source_target_pairs={{0,28},{4,0},{8,4},{12,8},{16,12},{20,16},{24,20},{28,24},{1,29},{... | collective-permute-start | bytes 1179656 | tf_op jit(solution)/shard_map/ppermute | solution.py:26
  26.5 11.1 %collective-permute-start.16 = (f32[2,6,64,128]{3,2,1,0:T(8,128)S(1)}, f32[2,6,64,128]{3,2,1,0:T(8,128)S(1)}, u32[]{:S(2)}, u32[]{:S(2)}) collective-permute-start(f32[2,6,64,128]{3,2,1,0:T(8,128)S(1)} %collective-permute-done.15), channel_id=1, source_target_pairs={{0,4},{4,8},{8,12},{12,16},{16,20},{20,24},{24,28},{28,0},{1,5},{5... | collective-permute-start | bytes 1179656 | tf_op jit(solution)/shard_map/ppermute | solution.py:26
  28.2 28.8 %copy-start = (f32[1,1,32,4096]{3,2,1,0:T(8,128)S(1)}, f32[1,1,32,4096]{3,2,1,0:T(8,128)}, u32[]{:S(2)}) copy-start(f32[1,1,32,4096]{3,2,1,0:T(8,128)} %param.4) | copy-start | bytes 1572868
  33.1 9.5 %collective-permute-start.13 = (f32[2,6,64,128]{3,2,1,0:T(8,128)S(1)}, f32[2,6,64,128]{3,2,1,0:T(8,128)S(1)}, u32[]{:S(2)}, u32[]{:S(2)}) collective-permute-start(f32[2,6,64,128]{3,2,1,0:T(8,128)S(1)} %collective-permute-done.12), channel_id=1, source_target_pairs={{0,28},{4,0},{8,4},{12,8},{16,12},{20,16},{24,20},{28,24},{1,29},{... | collective-permute-start | bytes 1179656 | tf_op jit(solution)/shard_map/ppermute | solution.py:26
  37.6 9.2 %collective-permute-start.17 = (f32[2,6,64,128]{3,2,1,0:T(8,128)S(1)}, f32[2,6,64,128]{3,2,1,0:T(8,128)S(1)}, u32[]{:S(2)}, u32[]{:S(2)}) collective-permute-start(f32[2,6,64,128]{3,2,1,0:T(8,128)S(1)} %collective-permute-done.16), channel_id=1, source_target_pairs={{0,4},{4,8},{8,12},{12,16},{16,20},{20,24},{24,28},{28,0},{1,5},{5... | collective-permute-start | bytes 1179656 | tf_op jit(solution)/shard_map/ppermute | solution.py:26
  42.6 7.0 %collective-permute-start.14 = (f32[6,64,128]{2,1,0:T(8,128)S(1)}, f32[6,64,128]{2,1,0:T(8,128)S(1)}, u32[]{:S(2)}, u32[]{:S(2)}) collective-permute-start(f32[6,64,128]{2,1,0:T(8,128)S(1)} %slice_bitcast_fusion.3), channel_id=1, source_target_pairs={{0,28},{4,0},{8,4},{12,8},{16,12},{20,16},{24,20},{28,24},{1,29},{... | collective-permute-start | bytes 589832 | tf_op jit(solution)/shard_map/ppermute | solution.py:26
  46.8 7.0 %collective-permute-start.18 = (f32[6,64,128]{2,1,0:T(8,128)S(1)}, f32[6,64,128]{2,1,0:T(8,128)S(1)}, u32[]{:S(2)}, u32[]{:S(2)}) collective-permute-start(f32[6,64,128]{2,1,0:T(8,128)S(1)} %slice_bitcast_fusion.2), channel_id=1, source_target_pairs={{0,4},{4,8},{8,12},{12,16},{16,20},{20,24},{24,28},{28,0},{1,5},{5... | collective-permute-start | bytes 589832 | tf_op jit(solution)/shard_map/ppermute | solution.py:26
  56.2 3.2 %copy-start.1 = (s32[1,1,32]{2,1,0:T(1,128)S(1)}, s32[1,1,32]{2,1,0:T(1,128)}, u32[]{:S(2)}) copy-start(s32[1,1,32]{2,1,0:T(1,128)} %param.6) | copy-start | bytes 388
  56.2 3.2 %copy-start.2 = (s32[1,1,32]{2,1,0:T(1,128)S(1)}, s32[1,1,32]{2,1,0:T(1,128)}, u32[]{:S(2)}) copy-start(s32[1,1,32]{2,1,0:T(1,128)} %param.5) | copy-start | bytes 388
  56.9 61.8 %collective-permute-start.19 = (f32[8,2,6,64,128]{4,3,2,1,0:T(8,128)}, f32[8,2,6,64,128]{4,3,2,1,0:T(8,128)}, u32[]{:S(2)}, u32[]{:S(2)}) collective-permute-start(f32[8,2,6,64,128]{4,3,2,1,0:T(8,128)} %bitcast_dynamic-update-slice_fusion), channel_id=1, source_target_pairs={{0,1},{1,0},{2,3},{3,2},{4,5},{5,4},{6,7},{7,6},{8,9},{9,8},{10,11... | collective-permute-start | bytes 9437192 | tf_op jit(solution)/shard_map/ppermute | solution.py:21
  58.8 17.8 %collective-permute-start.5 = (f32[16,64,128]{2,1,0:T(8,128)S(1)}, f32[16,64,128]{2,1,0:T(8,128)S(1)}, u32[]{:S(2)}, u32[]{:S(2)}) collective-permute-start(f32[16,64,128]{2,1,0:T(8,128)S(1)} %reshape.111), channel_id=1, source_target_pairs={{0,128},{128,0},{1,129},{129,1},{2,130},{130,2},{3,131},{131,3},{4... | collective-permute-start | bytes 1572872 | tf_op jit(solution)/shard_map/ppermute | solution.py:21
  59.4 13.8 %collective-permute-start = (s32[2,32]{1,0:T(2,128)S(1)}, s32[2,32]{1,0:T(2,128)S(1)}, u32[]{:S(2)}, u32[]{:S(2)}) collective-permute-start(s32[2,32]{1,0:T(2,128)S(1)} %get-tuple-element.12), channel_id=1, source_target_pairs={{0,128},{128,0},{1,129},{129,1},{2,130},{130,2},{3,131},{131,3},{4... | collective-permute-start | bytes 776 | tf_op jit(solution)/shard_map/ppermute | solution.py:21
  73.3 8.4 %collective-permute-start.1 = (s32[2,2,32]{2,1,0:T(2,128)S(1)}, s32[2,2,32]{2,1,0:T(2,128)S(1)}, u32[]{:S(2)}, u32[]{:S(2)}) collective-permute-start(s32[2,2,32]{2,1,0:T(2,128)S(1)} %pad_add_fusion), channel_id=1, source_target_pairs={{0,32},{32,64},{64,96},{96,0},{1,33},{33,65},{65,97},{97,1},{2,34}... | collective-permute-start | bytes 1544 | tf_op jit(solution)/shard_map/ppermute | solution.py:26
  74.8 3.9 %collective-permute-start.2 = (s32[2,2,32]{2,1,0:T(2,128)S(1)}, s32[2,2,32]{2,1,0:T(2,128)S(1)}, u32[]{:S(2)}, u32[]{:S(2)}) collective-permute-start(s32[2,2,32]{2,1,0:T(2,128)S(1)} %pad_add_fusion), channel_id=1, source_target_pairs={{0,96},{32,0},{64,32},{96,64},{1,97},{33,1},{65,33},{97,65},{2,98}... | collective-permute-start | bytes 1544 | tf_op jit(solution)/shard_map/ppermute | solution.py:26
  76.6 24.5 %collective-permute-start.7 = (f32[2,16,64,128]{3,2,1,0:T(8,128)S(1)}, f32[2,16,64,128]{3,2,1,0:T(8,128)S(1)}, u32[]{:S(2)}, u32[]{:S(2)}) collective-permute-start(f32[2,16,64,128]{3,2,1,0:T(8,128)S(1)} %pad_maximum_fusion), channel_id=1, source_target_pairs={{0,96},{32,0},{64,32},{96,64},{1,97},{33,1},{65,33},{97,65},{2,98}... | collective-permute-start | bytes 3145736 | tf_op jit(solution)/shard_map/ppermute | solution.py:26
  78.5 26.2 %collective-permute-start.6 = (f32[2,16,64,128]{3,2,1,0:T(8,128)S(1)}, f32[2,16,64,128]{3,2,1,0:T(8,128)S(1)}, u32[]{:S(2)}, u32[]{:S(2)}) collective-permute-start(f32[2,16,64,128]{3,2,1,0:T(8,128)S(1)} %pad_maximum_fusion), channel_id=1, source_target_pairs={{0,32},{32,64},{64,96},{96,0},{1,33},{33,65},{65,97},{97,1},{2,34}... | collective-permute-start | bytes 3145736 | tf_op jit(solution)/shard_map/ppermute | solution.py:26
  78.7 22.4 %collective-permute-start.3 = (s32[2,32]{1,0:T(2,128)S(1)}, s32[2,32]{1,0:T(2,128)S(1)}, u32[]{:S(2)}, u32[]{:S(2)}) collective-permute-start(s32[2,32]{1,0:T(2,128)S(1)} %slice_bitcast_fusion.5), channel_id=1, source_target_pairs={{0,96},{32,0},{64,32},{96,64},{1,97},{33,1},{65,33},{97,65},{2,98}... | collective-permute-start | bytes 776 | tf_op jit(solution)/shard_map/ppermute | solution.py:26
  81.7 23.8 %collective-permute-start.4 = (s32[2,32]{1,0:T(2,128)S(1)}, s32[2,32]{1,0:T(2,128)S(1)}, u32[]{:S(2)}, u32[]{:S(2)}) collective-permute-start(s32[2,32]{1,0:T(2,128)S(1)} %slice_bitcast_fusion.4), channel_id=1, source_target_pairs={{0,32},{32,64},{64,96},{96,0},{1,33},{33,65},{65,97},{97,1},{2,34}... | collective-permute-start | bytes 776 | tf_op jit(solution)/shard_map/ppermute | solution.py:26
  102.0 12.6 %collective-permute-start.8 = (f32[16,64,128]{2,1,0:T(8,128)}, f32[16,64,128]{2,1,0:T(8,128)}, u32[]{:S(2)}, u32[]{:S(2)}) collective-permute-start(f32[16,64,128]{2,1,0:T(8,128)} %slice_bitcast_fusion.1), channel_id=1, source_target_pairs={{0,96},{32,0},{64,32},{96,64},{1,97},{33,1},{65,33},{97,65},{2,98}... | collective-permute-start | bytes 1572872 | tf_op jit(solution)/shard_map/ppermute | solution.py:26
  105.5 13.2 %collective-permute-start.9 = (f32[16,64,128]{2,1,0:T(8,128)}, f32[16,64,128]{2,1,0:T(8,128)}, u32[]{:S(2)}, u32[]{:S(2)}) collective-permute-start(f32[16,64,128]{2,1,0:T(8,128)} %slice_bitcast_fusion), channel_id=1, source_target_pairs={{0,32},{32,64},{64,96},{96,0},{1,33},{33,65},{65,97},{97,1},{2,34}... | collective-permute-start | bytes 1572872 | tf_op jit(solution)/shard_map/ppermute | solution.py:26
